TPU v7x, 128 devices: a whole 4x4x4 slice. The times are simulated.
128 devices in a mesh: seq: 16 (over x, z_lo, core), heads: 8 (over z_hi, y).
Axes of the slice: x: 4, y: 4, z: 4 (z_hi: 2, z_lo: 2; z = z_hi * 2 + z_lo), core: 2. Of those that a mesh axis runs over, the one named last changes fastest.
Arguments:
- tokens: bfloat16 [4096, 5120], P('seq', 'heads'), may hold values from -6 to 6
- order: int32 [4096], replicated, may hold values from 0 to 4095, each once
- lengths: int32 [12], replicated, may hold values from 1 to 1024, 4096 in all
- block_table: int32 [12, 2], replicated, may hold values from 0 to 31, as said below
- destination: int32 [32], replicated, may hold values from 0 to 31, each once
- w_query: bfloat16 [5120, 5120], P(None, 'heads'), may hold values from -0.078125 to 0.078125
- key_weight: bfloat16 [5120, 1024], P(None, 'heads'), may hold values from -0.078125 to 0.078125
- value_weight: bfloat16 [5120, 1024], P(None, 'heads'), may hold values from -0.078125 to 0.078125
- w_out: bfloat16 [5120, 5120], P('heads'), may hold values from -0.078125 to 0.078125
- key_value_cache: bfloat16 [4, 32, 512, 2, 1024], P(None, None, 'seq', None, 'heads'), may hold values from -600 to 600
Outputs:
- attn_out: bfloat16 [4096, 5120], P('seq', 'heads')
- decode_cache: bfloat16 [4, 32, 512, 2, 1024], P(None, 'seq', None, None, 'heads')
Inputs may be any that keep to these rules, and one draw needn't show every extreme that they name: `block_table`: each of the 12 requests names 2 blocks; no block is named twice.
All inputs are finite; a program needn't handle non-finite values.
Results may differ from a plain program's by a relative error of at most 0.015.
The roundings to bfloat16 on the way count: a program that leaves them out, or rounds other values in their place, can miss the bound.
Values may be sent and summed in bfloat16 or wider, within the bound.
No kernel may reach another device: no remote copies, remote signals or barrier semaphores. Data moves between devices by JAX's collectives and lax.ppermute only.
A program may use at most 128 MiB of HBM per device.

v0:
```python
import jax
import jax.numpy as jnp
from jax import lax
from jax.sharding import PartitionSpec as P
import functools
from jax.experimental import pallas as pl
from jax.experimental.pallas import tpu as pltpu

QUERY_HEADS = 40
KEY_VALUE_HEADS = 8
HEAD_SIZE = 128
BLOCK_POSITIONS = 512
CB = 2


theta = 1000000.0
epsilon = 1e-06


def apply_rotary(value_rows, place):
    half = value_rows.shape[-1] // 2
    freq = theta ** (-2.0 * jnp.arange(half, dtype=jnp.float32) / value_rows.shape[-1])
    angle = place[:, None, None] * freq
    cosine = jnp.cos(angle)
    sine_part = jnp.sin(angle)
    first = value_rows[..., :half]
    second = value_rows[..., half:]
    return jnp.concatenate(
        [first * cosine - second * sine_part, second * cosine + first * sine_part], axis=-1
    )


def request_place(order, lengths):
    ends = jnp.cumsum(lengths)
    starts = ends - lengths
    request = jnp.sum((order[:, None] >= ends[None, :]).astype(jnp.int32), axis=1)
    labels = jnp.arange(lengths.shape[0], dtype=jnp.int32)
    begin = jnp.sum(jnp.where(request[:, None] == labels[None, :], starts[None, :], 0), axis=1)
    return (request, order - begin)


from jax.experimental import pallas as pl
from jax.experimental.pallas import tpu as pltpu

TILE = 32
CHUNK = 256


def _attn_body(tables, q_ref, o_ref, rs_ref, req_ref, kv_ref, cache_ref, out_ref, *, group, scale):
    t = pl.program_id(0)
    rows = q_ref.shape[1]
    size = q_ref.shape[2]
    q = q_ref[...].reshape(group * rows, size)
    o_row = o_ref[...]
    rs_row = rs_ref[...]
    req_row = req_ref[...]

    def update(carry, keys, values, mask):
        top, total, accum = carry
        width = keys.shape[0]
        scores = lax.dot_general(q, keys, (((1,), (1,)), ((), ())), preferred_element_type=jnp.float32) * scale
        scores = scores.reshape(group, rows, width)
        scores = jnp.where(mask[None], scores, -1e30).reshape(group * rows, width)
        new_top = jnp.maximum(top, jnp.max(scores, axis=1, keepdims=True))
        expo = jnp.exp(scores - new_top).reshape(group, rows, width)
        expo = jnp.where(mask[None], expo, 0.0).reshape(group * rows, width)
        fade = jnp.exp(top - new_top)
        total = total * fade + jnp.sum(expo, axis=1, keepdims=True)
        accum = accum * fade + jnp.dot(expo.astype(jnp.bfloat16), values, preferred_element_type=jnp.float32)
        return (new_top, total, accum)

    def cached(r, carry):
        mask = req_row == r
        for j in range(2):
            block = cache_ref[2 * r + j]
            carry = update(carry, block[:, :size], block[:, size:], mask)
        return carry

    def fresh(c, carry):
        start = pl.multiple_of(c * CHUNK, CHUNK)
        block = kv_ref[pl.ds(start, CHUNK), :]
        index = start + lax.broadcasted_iota(jnp.int32, (1, CHUNK), 1)
        mask = (index >= rs_row) & (index <= o_row)
        return update(carry, block[:, :size], block[:, size:], mask)

    carry = (
        jnp.full((group * rows, 1), -1e30, jnp.float32),
        jnp.zeros((group * rows, 1), jnp.float32),
        jnp.zeros((group * rows, size), jnp.float32),
    )
    carry = lax.fori_loop(tables[0, t], tables[1, t] + 1, cached, carry)
    carry = lax.fori_loop(tables[2, t], tables[3, t] + 1, fresh, carry)
    top, total, accum = carry
    out_ref[...] = (accum / total).reshape(group, rows, size).astype(out_ref.dtype)


def sparse_attention(q_sorted, o_sorted, rs_sorted, req_sorted, kv_sorted, cache, interpret=False):
    group, count, size = q_sorted.shape
    tiles = count // TILE
    firsts = jnp.arange(tiles) * TILE
    lasts = firsts + TILE - 1
    tables = jnp.stack([
        req_sorted[firsts], req_sorted[lasts], rs_sorted[firsts] // CHUNK, o_sorted[lasts] // CHUNK
    ]).astype(jnp.int32)
    col = lambda v: v.reshape(count, 1).astype(jnp.int32)
    body = functools.partial(_attn_body, group=group, scale=size ** (-0.5))
    spec = pltpu.PrefetchScalarGridSpec(
        num_scalar_prefetch=1,
        grid=(tiles,),
        in_specs=[
            pl.BlockSpec((group, TILE, size), lambda t, tb: (0, t, 0)),
            pl.BlockSpec((TILE, 1), lambda t, tb: (t, 0)),
            pl.BlockSpec((TILE, 1), lambda t, tb: (t, 0)),
            pl.BlockSpec((TILE, 1), lambda t, tb: (t, 0)),
            pl.BlockSpec(kv_sorted.shape, lambda t, tb: (0, 0)),
            pl.BlockSpec(cache.shape, lambda t, tb: (0, 0, 0)),
        ],
        out_specs=pl.BlockSpec((group, TILE, size), lambda t, tb: (0, t, 0)),
    )
    return pl.pallas_call(
        body,
        grid_spec=spec,
        out_shape=jax.ShapeDtypeStruct(q_sorted.shape, jnp.bfloat16),
        compiler_params=pltpu.CompilerParams(dimension_semantics=("arbitrary",)),
        interpret=interpret,
    )(tables, q_sorted, col(o_sorted), col(rs_sorted), col(req_sorted), kv_sorted, cache)


def rotate_columns(value, shift):
    doubled = jnp.concatenate([value, value], axis=1)
    return lax.dynamic_slice_in_dim(doubled, shift, value.shape[1], axis=1)


def gather_heads(piece):
    parts = lax.psum(1, "heads")
    me = lax.axis_index("heads")
    got = {0: piece}
    for shift in range(1, parts):
        pairs = [(i, (i + shift) % parts) for i in range(parts)]
        got[shift] = lax.ppermute(piece, "heads", pairs)
    ahead = jnp.concatenate([got[(parts - j) % parts] for j in range(parts)], axis=1)
    width = piece.shape[1]
    return rotate_columns(ahead, (parts - me) % parts * width)


def scatter_heads(partial_value):
    parts = lax.psum(1, "heads")
    me = lax.axis_index("heads")
    width = partial_value.shape[1] // parts
    ahead = rotate_columns(partial_value.astype(jnp.bfloat16), me * width)
    total = ahead[:, :width].astype(jnp.float32)
    for shift in range(1, parts):
        pairs = [(i, (i + shift) % parts) for i in range(parts)]
        piece = ahead[:, shift * width:(shift + 1) * width]
        total = total + lax.ppermute(piece, "heads", pairs).astype(jnp.float32)
    return total.astype(jnp.bfloat16)


def on_device(
    tokens,
    order,
    lengths,
    block_table,
    destination,
    w_query,
    key_weight,
    value_weight,
    w_out,
    key_value_cache,
):
    slots = destination.shape[0]
    slot_labels = jnp.arange(slots, dtype=jnp.int32)
    inverse = jnp.sum(
        jnp.where(destination[None, :] == slot_labels[:, None], slot_labels[None, :], 0), axis=1
    )
    arranged = jnp.take(key_value_cache, inverse, axis=1)
    decode_cache = lax.all_to_all(arranged, "seq", split_axis=1, concat_axis=2, tiled=True)
    full, decode_cache = lax.optimization_barrier((gather_heads(tokens), decode_cache))
    rows = full.shape[0]
    wide = full.astype(jnp.float32)
    normed = (wide * lax.rsqrt(jnp.mean(wide * wide, axis=1, keepdims=True) + epsilon)).astype(
        jnp.bfloat16
    )
    local_heads = key_weight.shape[1] // HEAD_SIZE
    head_group = QUERY_HEADS // KEY_VALUE_HEADS
    query_rows = jnp.dot(normed, w_query, preferred_element_type=jnp.float32)
    key_rows = jnp.dot(normed, key_weight, preferred_element_type=jnp.float32)
    value_rows = jnp.dot(normed, value_weight, preferred_element_type=jnp.float32)
    device = lax.axis_index("seq")
    my_order = lax.dynamic_slice_in_dim(order, device * rows, rows)
    request, position = request_place(my_order, lengths)
    rotary_angles = (position + CB * BLOCK_POSITIONS).astype(jnp.float32)
    query_rows = apply_rotary(
        query_rows.reshape(rows, local_heads * head_group, HEAD_SIZE), rotary_angles
    ).astype(jnp.bfloat16)
    query_rows = query_rows.reshape(rows, local_heads, head_group, HEAD_SIZE)
    key_rows = (
        apply_rotary(key_rows.reshape(rows, local_heads, HEAD_SIZE), rotary_angles)
        .astype(jnp.bfloat16)
        .reshape(rows, local_heads * HEAD_SIZE)
    )
    fresh_rows = jnp.concatenate(
        [
            key_rows.reshape(rows, local_heads, HEAD_SIZE),
            value_rows.astype(jnp.bfloat16).reshape(rows, local_heads, HEAD_SIZE),
        ],
        axis=2,
    ).reshape(rows, local_heads * 2 * HEAD_SIZE)
    gathered = lax.all_gather(fresh_rows, "seq", axis=0, tiled=True)
    kv_sorted = jnp.take(gathered, jnp.argsort(order), axis=0)
    layer_zero = key_value_cache[0]
    used = jnp.take(layer_zero, block_table.reshape(-1), axis=0)
    pool, span = used.shape[0], used.shape[1]
    used = used.reshape(pool, span, 2, local_heads, HEAD_SIZE).transpose(0, 1, 3, 2, 4)
    used = used.reshape(pool, span, local_heads * 2 * HEAD_SIZE)
    cache = lax.all_gather(used, "seq", axis=1, tiled=True)
    earlier = (my_order[None, :] < my_order[:, None]).astype(jnp.int32)
    unsort = jnp.sum(earlier, axis=1)
    slots_of = jnp.arange(rows, dtype=jnp.int32)
    perm = jnp.sum(jnp.where(unsort[:, None] == slots_of[None, :], slots_of[:, None], 0), axis=0)
    o_sorted = jnp.take(my_order, perm)
    rs_sorted = jnp.take(my_order - position, perm)
    req_sorted = jnp.take(request, perm)
    q_sorted = jnp.take(query_rows, perm, axis=0)
    outs = []
    for head in range(local_heads):
        result = sparse_attention(
            q_sorted[:, head].transpose(1, 0, 2),
            o_sorted,
            rs_sorted,
            req_sorted,
            kv_sorted[:, head * 2 * HEAD_SIZE:(head + 1) * 2 * HEAD_SIZE],
            cache[:, :, head * 2 * HEAD_SIZE:(head + 1) * 2 * HEAD_SIZE],
        )
        outs.append(jnp.take(result, unsort, axis=1).transpose(1, 0, 2))
    attn = jnp.stack(outs, axis=1).reshape(rows, local_heads * head_group * HEAD_SIZE)
    partial_value = jnp.dot(attn, w_out, preferred_element_type=jnp.float32)
    attn_out = scatter_heads(partial_value)
    return (attn_out, decode_cache)


def solution(mesh):
    placed = (
        P("seq", "heads"),
        P(),
        P(),
        P(),
        P(),
        P(None, "heads"),
        P(None, "heads"),
        P(None, "heads"),
        P("heads", None),
        P(None, None, "seq", None, "heads"),
    )
    return jax.shard_map(
        on_device,
        mesh=mesh,
        in_specs=placed,
        out_specs=(P("seq", "heads"), P(None, "seq", None, None, "heads")),
        check_vma=False,
    )
```

profile of v0, /device:TPU:0, one launch (start us, length us, event | category | flops | bytes accessed | tf_op | source)
XLA Modules:
  0.0 264.0 jit_solution(1619991029535614478)
XLA Ops:
  7.2 6.5 %collective-permute-start = (bf16[256,640]{1,0:T(8,128)(2,1)}, bf16[256,640]{1,0:T(8,128)(2,1)}, u32[]{:S(2)}, u32[]{:S(2)}) collective-permute-start(bf16[256,640]{1,0:T(8,128)(2,1)} %param.12), channel_id=1, source_target_pairs={{0,7},{1,0},{2,1},{3,2},{4,3},{5,4},{6,5},{7,6},{8,15},{9,8},{10,9... | collective-permute-start | bytes 983048 | tf_op jit(solution)/shard_map/ppermute | solution.py:140
  14.4 3.9 %collective-permute-start.3 = (bf16[256,640]{1,0:T(8,128)(2,1)}, bf16[256,640]{1,0:T(8,128)(2,1)}, u32[]{:S(2)}, u32[]{:S(2)}) collective-permute-start(bf16[256,640]{1,0:T(8,128)(2,1)} %param.12), channel_id=1, source_target_pairs={{0,4},{1,5},{2,6},{3,7},{4,0},{5,1},{6,2},{7,3},{8,12},{9,13},{10,... | collective-permute-start | bytes 983048 | tf_op jit(solution)/shard_map/ppermute | solution.py:140
  19.1 7.0 %gather_fusion.4 = bf16[32,4,32,2,128]{4,3,2,1,0:T(2,128)(2,1)S(1)} fusion(bf16[4,32,32,2,128]{4,3,2,1,0:T(2,128)(2,1)} %param.21, s32[1024]{0:T(1024)S(1)} %pad_clamp_fusion.3), kind=kCustom, calls=%fused_computation.7 | custom fusion | bytes 4194432 | tf_op jit(solution)/shard_map/jit(_take)/gather | solution.py:176
  26.1 3.2 %fusion.3 = bf16[4,32,32,2,128]{4,3,2,0,1:T(2,128)(2,1)} fusion(bf16[32,4,32,2,128]{4,3,2,1,0:T(2,128)(2,1)S(1)} %gather_fusion.4, pred[32]{0:T(512)(128)(4,1)S(1)} %compare_and_fusion.3), kind=kLoop, calls=%fused_computation.21 | loop fusion | flops 1048576 | bytes 4194336 | tf_op jit(solution)/shard_map/jit(_take)/select_n | solution.py:176
  29.4 4.9 %all-to-all-start = ((bf16[4,32,32,2,128]{4,3,2,0,1:T(2,128)(2,1)}), bf16[4,32,32,2,128]{4,3,2,0,1:T(2,128)(2,1)S(1)}, u32[]{:S(2)}, u32[]{:S(2)}) async-start(bf16[4,32,32,2,128]{4,3,2,0,1:T(2,128)(2,1)} %fusion.3), calls=%async_computation | async-start | bytes 4194304 | tf_op jit(solution)/shard_map/all_to_all | solution.py:177
  36.0 4.0 %collective-permute-start.5 = (bf16[256,640]{1,0:T(8,128)(2,1)}, bf16[256,640]{1,0:T(8,128)(2,1)S(1)}, u32[]{:S(2)}, u32[]{:S(2)}) collective-permute-start(bf16[256,640]{1,0:T(8,128)(2,1)} %param.12), channel_id=1, source_target_pairs={{0,2},{1,3},{2,4},{3,5},{4,6},{5,7},{6,0},{7,1},{8,10},{9,11},{10,... | collective-permute-start | bytes 983048 | tf_op jit(solution)/shard_map/ppermute | solution.py:140
  45.5 13.8 %collective-permute-done.5 = bf16[256,640]{1,0:T(8,128)(2,1)S(1)} collective-permute-done((bf16[256,640]{1,0:T(8,128)(2,1)}, bf16[256,640]{1,0:T(8,128)(2,1)S(1)}, u32[]{:S(2)}, u32[]{:S(2)}) %collective-permute-start.5) | collective-permute-done | bytes 327712 | tf_op jit(solution)/shard_map/ppermute | solution.py:140
  59.4 15.3 %collective-permute-done.6 = bf16[256,640]{1,0:T(8,128)(2,1)S(1)} collective-permute-done((bf16[256,640]{1,0:T(8,128)(2,1)}, bf16[256,640]{1,0:T(8,128)(2,1)S(1)}, u32[]{:S(2)}, u32[]{:S(2)}) %collective-permute-start.6) | collective-permute-done | bytes 327712 | tf_op jit(solution)/shard_map/ppermute | solution.py:140
  80.1 1.8 constant_dynamic-slice_fusion
  81.9 3.3 %copy.30 = bf16[4,16,2,32,2,128]{5,4,3,1,2,0:T(2,128)(2,1)} copy(bf16[4,16,2,32,2,128]{5,4,3,0,2,1:T(2,128)(2,1)S(1)} %bitcast.69) | data formatting | bytes 4194304 | tf_op jit(solution)/shard_map/all_to_all | solution.py:177
  89.7 1.5 slice_bitcast_fusion
  91.2 1.3 gather_fusion.7
  94.0 1.9 gather_fusion.9
  96.0 1.9 gather_fusion.10
  97.9 1.9 gather_fusion.11
  99.9 5.8 %sort.17 = (s32[4096]{0:T(1024)}, s32[4096]{0:T(1024)S(1)}) sort(s32[4096]{0:T(1024)S(1)} %copy-done.4, s32[4096]{0:T(1024)S(1)} %iota.43), dimensions={0}, to_apply=%region_7.9 | sort | flops 49152 | bytes 65536 | tf_op jit(solution)/shard_map/jit(argsort)/sort | solution.py:210
  111.9 6.5 %fusion.23 = f32[256,640]{0,1:T(8,128)S(1)} fusion(bf16[5120,640]{1,0:T(8,128)(2,1)} %param.17, bf16[256,5120]{1,0:T(8,128)(2,1)} %constant_dynamic-slice_fusion, f32[256]{0:T(256)S(1)} %add_rsqrt_fusion), kind=kOutput, calls=%fused_computation.122 | convolution fusion | flops 1681653760 | bytes 9831424 | tf_op jit(solution)/shard_map/dot_general | solution.py:186
  121.7 3.3 %copy.35 = bf16[4096,256]{1,0:T(8,128)(2,1)S(1)} copy(bf16[4096,256]{0,1:T(8,128)(2,1)} %bitcast.71) | data formatting | bytes 4194304 | tf_op jit(solution)/shard_map/all_gather | solution.py:209
  124.9 17.0 %gather_fusion.6 = bf16[4096,256]{1,0:T(8,128)(2,1)} fusion(bf16[4096,256]{1,0:T(8,128)(2,1)S(1)} %copy.35, s32[4096]{0:T(1024)S(1)} %fusion.16), kind=kCustom, calls=%fused_computation.9 | custom fusion | bytes 4210688 | tf_op jit(solution)/shard_map/jit(_take)/gather | solution.py:210
  142.0 3.0 %broadcast_select_fusion.1.kv_ref = bf16[4096,256]{1,0:T(8,128)(2,1)} fusion(bf16[4096,256]{1,0:T(8,128)(2,1)} %gather_fusion.6, pred[4096]{0:T(1024)(128)(4,1)S(1)} %compare_and_fusion), kind=kLoop, calls=%fused_computation.22 | loop fusion | flops 1048576 | bytes 4198400 | tf_op jit(solution)/shard_map/jit(_take)/select_n | solution.py:210
  144.9 20.3 %all-gather.4.cloned.1.call-done.cache_ref = bf16[24,512,256]{2,1,0:T(8,128)(2,1)} async-done(((bf16[24,32,256]{2,1,0:T(8,128)(2,1)}), bf16[24,512,256]{2,1,0:T(8,128)(2,1)}) %all-gather.4.cloned.1.call-update) | async-done | bytes 6291472 | tf_op jit(solution)/shard_map/all_gather | solution.py:216
  165.3 32.7 %shard_map.113 = bf16[5,256,128]{2,1,0:T(8,128)(2,1)} custom-call(s32[4,8]{1,0:T(4,128)} %pad_add_fusion.tables, bf16[5,256,128]{2,1,0:T(8,128)(2,1)} %fusion.7.q_ref, s32[256,1]{1,0:T(8,128)} %copy.38.o_ref, s32[256,1]{1,0:T(8,128)} %copy.39.rs_ref, s32[256,1]{1,0:T(8,128)} %copy.40.req_ref, bf16[4096,256]{1,0:T(8,128)(2,1)} %broadcast_select_fusion.1.kv_ref, ...), custom_call_target="tpu_custom_call" | custom-call | tf_op jit(solution)/shard_map/pallas_call | solution.py:120
  200.3 5.2 %convolution_convert_fusion = bf16[256,5120]{1,0:T(8,128)(2,1)S(1)} fusion(bf16[256,640]{0,1:T(8,128)(2,1)S(1)} %bitcast.72, bf16[640,5120]{1,0:T(8,128)(2,1)} %param.20), kind=kOutput, calls=%fused_computation.14 | convolution fusion | flops 1679032320 | bytes 9502720 | tf_op jit(solution)/shard_map/dot_general | solution.py:237
  205.5 1.4 fusion.2
  207.2 2.9 %collective-permute-start.10 = (bf16[256,640]{1,0:T(8,128)(2,1)S(1)}, bf16[256,640]{1,0:T(8,128)(2,1)S(1)}, u32[]{:S(2)}, u32[]{:S(2)}) collective-permute-start(bf16[256,640]{1,0:T(8,128)(2,1)S(1)} %get-tuple-element.14), channel_id=1, source_target_pairs={{0,4},{1,5},{2,6},{3,7},{4,0},{5,1},{6,2},{7,3},{8,12},{9,13},{10,... | collective-permute-start | bytes 983048 | tf_op jit(solution)/shard_map/ppermute | solution.py:155
  210.1 1.6 collective-permute-start.11
  211.7 5.0 %collective-permute-start.12 = (bf16[256,640]{1,0:T(8,128)(2,1)S(1)}, bf16[256,640]{1,0:T(8,128)(2,1)S(1)}, u32[]{:S(2)}, u32[]{:S(2)}) collective-permute-start(bf16[256,640]{1,0:T(8,128)(2,1)S(1)} %get-tuple-element.12), channel_id=1, source_target_pairs={{0,6},{1,7},{2,0},{3,1},{4,2},{5,3},{6,4},{7,5},{8,14},{9,15},{10,... | collective-permute-start | bytes 983048 | tf_op jit(solution)/shard_map/ppermute | solution.py:155
  216.7 1.4 collective-permute-start.13
  218.7 13.7 %collective-permute-start.8 = (bf16[256,640]{1,0:T(8,128)(2,1)S(1)}, bf16[256,640]{1,0:T(8,128)(2,1)S(1)}, u32[]{:S(2)}, u32[]{:S(2)}) collective-permute-start(bf16[256,640]{1,0:T(8,128)(2,1)S(1)} %get-tuple-element.16), channel_id=1, source_target_pairs={{0,2},{1,3},{2,4},{3,5},{4,6},{5,7},{6,0},{7,1},{8,10},{9,11},{10,... | collective-permute-start | bytes 983048 | tf_op jit(solution)/shard_map/ppermute | solution.py:155
  232.4 7.2 %collective-permute-start.9 = (bf16[256,640]{1,0:T(8,128)(2,1)S(1)}, bf16[256,640]{1,0:T(8,128)(2,1)S(1)}, u32[]{:S(2)}, u32[]{:S(2)}) collective-permute-start(bf16[256,640]{1,0:T(8,128)(2,1)S(1)} %get-tuple-element.15), channel_id=1, source_target_pairs={{0,3},{1,4},{2,5},{3,6},{4,7},{5,0},{6,1},{7,2},{8,11},{9,12},{10,... | collective-permute-start | bytes 983048 | tf_op jit(solution)/shard_map/ppermute | solution.py:155
  239.6 6.2 %collective-permute-done.8 = bf16[256,640]{1,0:T(8,128)(2,1)S(1)} collective-permute-done((bf16[256,640]{1,0:T(8,128)(2,1)S(1)}, bf16[256,640]{1,0:T(8,128)(2,1)S(1)}, u32[]{:S(2)}, u32[]{:S(2)}) %collective-permute-start.8) | collective-permute-done | bytes 327712 | tf_op jit(solution)/shard_map/ppermute | solution.py:155
  245.9 10.3 %collective-permute-done.9 = bf16[256,640]{1,0:T(8,128)(2,1)S(1)} collective-permute-done((bf16[256,640]{1,0:T(8,128)(2,1)S(1)}, bf16[256,640]{1,0:T(8,128)(2,1)S(1)}, u32[]{:S(2)}, u32[]{:S(2)}) %collective-permute-start.9) | collective-permute-done | bytes 327712 | tf_op jit(solution)/shard_map/ppermute | solution.py:155
  (118 shorter events, 33.4 us)
Async XLA Ops:
  7.2 78.7 %copy-start = (bf16[5120,128]{1,0:T(8,128)(2,1)S(1)}, bf16[5120,128]{1,0:T(8,128)(2,1)}, u32[]{:S(2)}) copy-start(bf16[5120,128]{1,0:T(8,128)(2,1)} %param.18) | copy-start | bytes 3932164
  7.2 28.8 %collective-permute-start = (bf16[256,640]{1,0:T(8,128)(2,1)}, bf16[256,640]{1,0:T(8,128)(2,1)}, u32[]{:S(2)}, u32[]{:S(2)}) collective-permute-start(bf16[256,640]{1,0:T(8,128)(2,1)} %param.12), channel_id=1, source_target_pairs={{0,7},{1,0},{2,1},{3,2},{4,3},{5,4},{6,5},{7,6},{8,15},{9,8},{10,9... | collective-permute-start | bytes 983048 | tf_op jit(solution)/shard_map/ppermute | solution.py:140
  13.7 27.3 %collective-permute-start.1 = (bf16[256,640]{1,0:T(8,128)(2,1)}, bf16[256,640]{1,0:T(8,128)(2,1)}, u32[]{:S(2)}, u32[]{:S(2)}) collective-permute-start(bf16[256,640]{1,0:T(8,128)(2,1)} %param.12), channel_id=1, source_target_pairs={{0,6},{1,7},{2,0},{3,1},{4,2},{5,3},{6,4},{7,5},{8,14},{9,15},{10,... | collective-permute-start | bytes 983048 | tf_op jit(solution)/shard_map/ppermute | solution.py:140
  14.3 28.0 %collective-permute-start.2 = (bf16[256,640]{1,0:T(8,128)(2,1)}, bf16[256,640]{1,0:T(8,128)(2,1)}, u32[]{:S(2)}, u32[]{:S(2)}) collective-permute-start(bf16[256,640]{1,0:T(8,128)(2,1)} %param.12), channel_id=1, source_target_pairs={{0,5},{1,6},{2,7},{3,0},{4,1},{5,2},{6,3},{7,4},{8,13},{9,14},{10,... | collective-permute-start | bytes 983048 | tf_op jit(solution)/shard_map/ppermute | solution.py:140
  14.4 29.0 %collective-permute-start.3 = (bf16[256,640]{1,0:T(8,128)(2,1)}, bf16[256,640]{1,0:T(8,128)(2,1)}, u32[]{:S(2)}, u32[]{:S(2)}) collective-permute-start(bf16[256,640]{1,0:T(8,128)(2,1)} %param.12), channel_id=1, source_target_pairs={{0,4},{1,5},{2,6},{3,7},{4,0},{5,1},{6,2},{7,3},{8,12},{9,13},{10,... | collective-permute-start | bytes 983048 | tf_op jit(solution)/shard_map/ppermute | solution.py:140
  18.3 26.2 %collective-permute-start.4 = (bf16[256,640]{1,0:T(8,128)(2,1)}, bf16[256,640]{1,0:T(8,128)(2,1)}, u32[]{:S(2)}, u32[]{:S(2)}) collective-permute-start(bf16[256,640]{1,0:T(8,128)(2,1)} %param.12), channel_id=1, source_target_pairs={{0,3},{1,4},{2,5},{3,6},{4,7},{5,0},{6,1},{7,2},{8,11},{9,12},{10,... | collective-permute-start | bytes 983048 | tf_op jit(solution)/shard_map/ppermute | solution.py:140
  26.1 8.2 %copy-start.7 = (s32[12]{0:T(128)S(1)}, s32[12]{0:T(128)}, u32[]{:S(2)}) copy-start(s32[12]{0:T(128)} %param.14) | copy-start | bytes 148
  26.1 8.4 %copy-start.4 = (s32[4096]{0:T(1024)S(1)}, s32[4096]{0:T(1024)}, u32[]{:S(2)}) copy-start(s32[4096]{0:T(1024)} %param.13) | copy-start | bytes 49156
  29.4 52.5 %all-to-all-start = ((bf16[4,32,32,2,128]{4,3,2,0,1:T(2,128)(2,1)}), bf16[4,32,32,2,128]{4,3,2,0,1:T(2,128)(2,1)S(1)}, u32[]{:S(2)}, u32[]{:S(2)}) async-start(bf16[4,32,32,2,128]{4,3,2,0,1:T(2,128)(2,1)} %fusion.3), calls=%async_computation | async-start | bytes 4194304 | tf_op jit(solution)/shard_map/all_to_all | solution.py:177
  34.2 87.4 %all-gather.6.cloned.1.call-start = ((), (), s32[]{:S(2)}) async-start(), calls=%async_computation.2 | async-start | bytes 2228224 | tf_op jit(solution)/shard_map/all_gather | solution.py:209
  34.8 39.9 %copy-start.3 = (bf16[256,640]{1,0:T(8,128)(2,1)S(1)}, bf16[256,640]{1,0:T(8,128)(2,1)}, u32[]{:S(2)}) copy-start(bf16[256,640]{1,0:T(8,128)(2,1)} %param.12) | copy-start | bytes 983044
  36.0 23.3 %collective-permute-start.5 = (bf16[256,640]{1,0:T(8,128)(2,1)}, bf16[256,640]{1,0:T(8,128)(2,1)S(1)}, u32[]{:S(2)}, u32[]{:S(2)}) collective-permute-start(bf16[256,640]{1,0:T(8,128)(2,1)} %param.12), channel_id=1, source_target_pairs={{0,2},{1,3},{2,4},{3,5},{4,6},{5,7},{6,0},{7,1},{8,10},{9,11},{10,... | collective-permute-start | bytes 983048 | tf_op jit(solution)/shard_map/ppermute | solution.py:140
  41.0 33.6 %collective-permute-start.6 = (bf16[256,640]{1,0:T(8,128)(2,1)}, bf16[256,640]{1,0:T(8,128)(2,1)S(1)}, u32[]{:S(2)}, u32[]{:S(2)}) collective-permute-start(bf16[256,640]{1,0:T(8,128)(2,1)} %param.12), channel_id=1, source_target_pairs={{0,1},{1,2},{2,3},{3,4},{4,5},{5,6},{6,7},{7,0},{8,9},{9,10},{10,1... | collective-permute-start | bytes 983048 | tf_op jit(solution)/shard_map/ppermute | solution.py:140
  81.9 3.3 %copy-start.2 = (bf16[256,5120]{1,0:T(8,128)(2,1)S(1)}, bf16[256,5120]{1,0:T(8,128)(2,1)}, u32[]{:S(2)}) copy-start(bf16[256,5120]{1,0:T(8,128)(2,1)} %constant_dynamic-slice_fusion) | copy-start | bytes 7864324
  81.9 5.1 %copy-start.6 = (bf16[5120,128]{1,0:T(8,128)(2,1)S(1)}, bf16[5120,128]{1,0:T(8,128)(2,1)}, u32[]{:S(2)}) copy-start(bf16[5120,128]{1,0:T(8,128)(2,1)} %param.19) | copy-start | bytes 3932164
  85.8 3.6 %copy-start.5 = (s32[12,2]{0,1:T(2,128)S(1)}, s32[12,2]{0,1:T(2,128)}, u32[]{:S(2)}) copy-start(s32[12,2]{0,1:T(2,128)} %param.15) | copy-start | bytes 292
  89.1 76.2 %all-gather.4.cloned.1.call-start = ((), (), s32[]{:S(2)}) async-start(), calls=%async_computation.1 | async-start | bytes 6684672 | tf_op jit(solution)/shard_map/all_gather | solution.py:216
  200.3 56.9 %copy-start.1 = (bf16[5120,128]{1,0:T(8,128)(2,1)S(1)}, bf16[5120,128]{1,0:T(8,128)(2,1)}, u32[]{:S(2)}) copy-start(bf16[5120,128]{1,0:T(8,128)(2,1)} %param.18) | copy-start | bytes 3932164
  207.2 11.6 %collective-permute-start.10 = (bf16[256,640]{1,0:T(8,128)(2,1)S(1)}, bf16[256,640]{1,0:T(8,128)(2,1)S(1)}, u32[]{:S(2)}, u32[]{:S(2)}) collective-permute-start(bf16[256,640]{1,0:T(8,128)(2,1)S(1)} %get-tuple-element.14), channel_id=1, source_target_pairs={{0,4},{1,5},{2,6},{3,7},{4,0},{5,1},{6,2},{7,3},{8,12},{9,13},{10,... | collective-permute-start | bytes 983048 | tf_op jit(solution)/shard_map/ppermute | solution.py:155
  210.1 22.4 %collective-permute-start.11 = (bf16[256,640]{1,0:T(8,128)(2,1)S(1)}, bf16[256,640]{1,0:T(8,128)(2,1)S(1)}, u32[]{:S(2)}, u32[]{:S(2)}) collective-permute-start(bf16[256,640]{1,0:T(8,128)(2,1)S(1)} %get-tuple-element.13), channel_id=1, source_target_pairs={{0,5},{1,6},{2,7},{3,0},{4,1},{5,2},{6,3},{7,4},{8,13},{9,14},{10,... | collective-permute-start | bytes 983048 | tf_op jit(solution)/shard_map/ppermute | solution.py:155
  211.7 27.9 %collective-permute-start.12 = (bf16[256,640]{1,0:T(8,128)(2,1)S(1)}, bf16[256,640]{1,0:T(8,128)(2,1)S(1)}, u32[]{:S(2)}, u32[]{:S(2)}) collective-permute-start(bf16[256,640]{1,0:T(8,128)(2,1)S(1)} %get-tuple-element.12), channel_id=1, source_target_pairs={{0,6},{1,7},{2,0},{3,1},{4,2},{5,3},{6,4},{7,5},{8,14},{9,15},{10,... | collective-permute-start | bytes 983048 | tf_op jit(solution)/shard_map/ppermute | solution.py:155
  216.7 22.9 %collective-permute-start.13 = (bf16[256,640]{1,0:T(8,128)(2,1)S(1)}, bf16[256,640]{1,0:T(8,128)(2,1)S(1)}, u32[]{:S(2)}, u32[]{:S(2)}) collective-permute-start(bf16[256,640]{1,0:T(8,128)(2,1)S(1)} %get-tuple-element.17), channel_id=1, source_target_pairs={{0,7},{1,0},{2,1},{3,2},{4,3},{5,4},{6,5},{7,6},{8,15},{9,8},{10,9... | collective-permute-start | bytes 983048 | tf_op jit(solution)/shard_map/ppermute | solution.py:155
  218.1 21.5 %collective-permute-start.7 = (bf16[256,640]{1,0:T(8,128)(2,1)S(1)}, bf16[256,640]{1,0:T(8,128)(2,1)S(1)}, u32[]{:S(2)}, u32[]{:S(2)}) collective-permute-start(bf16[256,640]{1,0:T(8,128)(2,1)S(1)} %get-tuple-element.11), channel_id=1, source_target_pairs={{0,1},{1,2},{2,3},{3,4},{4,5},{5,6},{6,7},{7,0},{8,9},{9,10},{10,1... | collective-permute-start | bytes 983048 | tf_op jit(solution)/shard_map/ppermute | solution.py:155
  218.7 27.1 %collective-permute-start.8 = (bf16[256,640]{1,0:T(8,128)(2,1)S(1)}, bf16[256,640]{1,0:T(8,128)(2,1)S(1)}, u32[]{:S(2)}, u32[]{:S(2)}) collective-permute-start(bf16[256,640]{1,0:T(8,128)(2,1)S(1)} %get-tuple-element.16), channel_id=1, source_target_pairs={{0,2},{1,3},{2,4},{3,5},{4,6},{5,7},{6,0},{7,1},{8,10},{9,11},{10,... | collective-permute-start | bytes 983048 | tf_op jit(solution)/shard_map/ppermute | solution.py:155
  232.4 23.7 %collective-permute-start.9 = (bf16[256,640]{1,0:T(8,128)(2,1)S(1)}, bf16[256,640]{1,0:T(8,128)(2,1)S(1)}, u32[]{:S(2)}, u32[]{:S(2)}) collective-permute-start(bf16[256,640]{1,0:T(8,128)(2,1)S(1)} %get-tuple-element.15), channel_id=1, source_target_pairs={{0,3},{1,4},{2,5},{3,6},{4,7},{5,0},{6,1},{7,2},{8,11},{9,12},{10,... | collective-permute-start | bytes 983048 | tf_op jit(solution)/shard_map/ppermute | solution.py:155
Sparse Core Ops, SparseCore 0:
  89.2 32.3 all-gather.5
  123.3 41.9 all-gather.3
where the time goes:
time: 268 us; the launch traced here: 264 us
  waiting for transfers between devices  66 us (25%)
  local copies, waits for them, and re-layouts  62.5 us (23%)
  starting transfers between devices  52.9 us (20%)
  Pallas kernels  32.7 us (12%)
  other arithmetic  21.3 us (8%)
  between operations  14.6 us (5%)
  matrix products  14 us (5%)
    pallas_call x1, Pallas kernels, sparse_attention(): pl.pallas_call(body, grid_spec=spec, out_shape=jax.ShapeDtypeStruct(q_sor...  32.7 us
    ppermute x7, starting transfers between devices, scatter_heads(): total = total + lax.ppermute(piece, 'heads', pairs).astype(jnp.float32)  32.4 us
    ppermute x7, waiting for transfers between devices, gather_heads(): got[shift] = lax.ppermute(piece, 'heads', pairs)  29.1 us
    all_gather x1, waiting for transfers between devices, on_device(): cache = lax.all_gather(used, 'seq', axis=1, tiled=True)  20.3 us
    gather x1, local copies, waits for them, and re-layouts, on_device(): kv_sorted = jnp.take(gathered, jnp.argsort(order), axis=0)  17 us
    ppermute x7, waiting for transfers between devices, scatter_heads(): total = total + lax.ppermute(piece, 'heads', pairs).astype(jnp.float32)  16.5 us
    ppermute x7, starting transfers between devices, gather_heads(): got[shift] = lax.ppermute(piece, 'heads', pairs)  15.3 us
    unnamed x34, local copies, waits for them, and re-layouts  12.5 us
  transfers between devices with their start and end apart: 17, of which 5 were waited for; matrix products, arithmetic and copies ran while one was open for 30% of the time, Pallas kernels for 0%

commit v1 on v0

--- a/solution.py
+++ b/solution.py
@@ -46,74 +46,117 @@
 CHUNK = 256
 
 
-def _attn_body(tables, q_ref, o_ref, rs_ref, req_ref, kv_ref, cache_ref, out_ref, *, group, scale):
+def _online(q, keys, values, mask, carry, scale):
+    top, total, accum = carry
+    width = keys.shape[0]
+    scores = lax.dot_general(q, keys, (((1,), (1,)), ((), ())), preferred_element_type=jnp.float32) * scale
+    scores = scores.reshape(-1, mask.shape[0], width)
+    scores = jnp.where(mask[None], scores, -1e30).reshape(q.shape[0], width)
+    new_top = jnp.maximum(top, jnp.max(scores, axis=1, keepdims=True))
+    expo = jnp.exp(scores - new_top).reshape(-1, mask.shape[0], width)
+    expo = jnp.where(mask[None], expo, 0.0).reshape(q.shape[0], width)
+    fade = jnp.exp(top - new_top)
+    total = total * fade + jnp.sum(expo, axis=1, keepdims=True)
+    accum = accum * fade + jnp.dot(expo.astype(jnp.bfloat16), values, preferred_element_type=jnp.float32)
+    return (new_top, total, accum)
+
+
+def _cache_body(tables, q_ref, req_ref, cache_ref, top_ref, total_ref, accum_ref, *, scale):
     t = pl.program_id(0)
-    rows = q_ref.shape[1]
-    size = q_ref.shape[2]
+    group, rows, size = q_ref.shape
     q = q_ref[...].reshape(group * rows, size)
-    o_row = o_ref[...]
-    rs_row = rs_ref[...]
     req_row = req_ref[...]
-
-    def update(carry, keys, values, mask):
-        top, total, accum = carry
-        width = keys.shape[0]
-        scores = lax.dot_general(q, keys, (((1,), (1,)), ((), ())), preferred_element_type=jnp.float32) * scale
-        scores = scores.reshape(group, rows, width)
-        scores = jnp.where(mask[None], scores, -1e30).reshape(group * rows, width)
-        new_top = jnp.maximum(top, jnp.max(scores, axis=1, keepdims=True))
-        expo = jnp.exp(scores - new_top).reshape(group, rows, width)
-        expo = jnp.where(mask[None], expo, 0.0).reshape(group * rows, width)
-        fade = jnp.exp(top - new_top)
-        total = total * fade + jnp.sum(expo, axis=1, keepdims=True)
-        accum = accum * fade + jnp.dot(expo.astype(jnp.bfloat16), values, preferred_element_type=jnp.float32)
-        return (new_top, total, accum)
 
     def cached(r, carry):
         mask = req_row == r
         for j in range(2):
             block = cache_ref[2 * r + j]
-            carry = update(carry, block[:, :size], block[:, size:], mask)
+            carry = _online(q, block[:, :size], block[:, size:], mask, carry, scale)
         return carry
+
+    carry = (
+        jnp.full((group * rows, 1), -1e30, jnp.float32),
+        jnp.zeros((group * rows, 1), jnp.float32),
+        jnp.zeros((group * rows, size), jnp.float32),
+    )
+    top, total, accum = lax.fori_loop(tables[0, t], tables[1, t] + 1, cached, carry)
+    top_ref[...] = top
+    total_ref[...] = total
+    accum_ref[...] = accum
+
+
+def _fresh_body(tables, q_ref, o_ref, rs_ref, top_ref, total_ref, accum_ref, kv_ref, out_ref, *, scale):
+    t = pl.program_id(0)
+    group, rows, size = q_ref.shape
+    q = q_ref[...].reshape(group * rows, size)
+    o_row = o_ref[...]
+    rs_row = rs_ref[...]
 
     def fresh(c, carry):
         start = pl.multiple_of(c * CHUNK, CHUNK)
         block = kv_ref[pl.ds(start, CHUNK), :]
         index = start + lax.broadcasted_iota(jnp.int32, (1, CHUNK), 1)
         mask = (index >= rs_row) & (index <= o_row)
-        return update(carry, block[:, :size], block[:, size:], mask)
-
-    carry = (
-        jnp.full((group * rows, 1), -1e30, jnp.float32),
-        jnp.zeros((group * rows, 1), jnp.float32),
-        jnp.zeros((group * rows, size), jnp.float32),
-    )
-    carry = lax.fori_loop(tables[0, t], tables[1, t] + 1, cached, carry)
-    carry = lax.fori_loop(tables[2, t], tables[3, t] + 1, fresh, carry)
-    top, total, accum = carry
+        return _online(q, block[:, :size], block[:, size:], mask, carry, scale)
+
+    carry = (top_ref[...], total_ref[...], accum_ref[...])
+    top, total, accum = lax.fori_loop(tables[2, t], tables[3, t] + 1, fresh, carry)
     out_ref[...] = (accum / total).reshape(group, rows, size).astype(out_ref.dtype)
 
 
-def sparse_attention(q_sorted, o_sorted, rs_sorted, req_sorted, kv_sorted, cache, interpret=False):
+def attention_tables(o_sorted, rs_sorted, req_sorted):
+    count = o_sorted.shape[0]
+    firsts = jnp.arange(count // TILE) * TILE
+    lasts = firsts + TILE - 1
+    return jnp.stack([
+        req_sorted[firsts], req_sorted[lasts], rs_sorted[firsts] // CHUNK, o_sorted[lasts] // CHUNK
+    ]).astype(jnp.int32)
+
+
+def cache_attention(tables, q_sorted, req_sorted, cache):
     group, count, size = q_sorted.shape
     tiles = count // TILE
-    firsts = jnp.arange(tiles) * TILE
-    lasts = firsts + TILE - 1
-    tables = jnp.stack([
-        req_sorted[firsts], req_sorted[lasts], rs_sorted[firsts] // CHUNK, o_sorted[lasts] // CHUNK
-    ]).astype(jnp.int32)
-    col = lambda v: v.reshape(count, 1).astype(jnp.int32)
-    body = functools.partial(_attn_body, group=group, scale=size ** (-0.5))
+    body = functools.partial(_cache_body, scale=size ** (-0.5))
+    state = pl.BlockSpec((group * TILE, 1), lambda t, tb: (t, 0))
     spec = pltpu.PrefetchScalarGridSpec(
         num_scalar_prefetch=1,
         grid=(tiles,),
         in_specs=[
             pl.BlockSpec((group, TILE, size), lambda t, tb: (0, t, 0)),
             pl.BlockSpec((TILE, 1), lambda t, tb: (t, 0)),
-            pl.BlockSpec((TILE, 1), lambda t, tb: (t, 0)),
-            pl.BlockSpec((TILE, 1), lambda t, tb: (t, 0)),
+            pl.BlockSpec(cache.shape, lambda t, tb: (0, 0, 0)),
+        ],
+        out_specs=[state, state, pl.BlockSpec((group * TILE, size), lambda t, tb: (t, 0))],
+    )
+    return pl.pallas_call(
+        body,
+        grid_spec=spec,
+        out_shape=[
+            jax.ShapeDtypeStruct((group * count, 1), jnp.float32),
+            jax.ShapeDtypeStruct((group * count, 1), jnp.float32),
+            jax.ShapeDtypeStruct((group * count, size), jnp.float32),
+        ],
+        compiler_params=pltpu.CompilerParams(dimension_semantics=("arbitrary",)),
+    )(tables, q_sorted, req_sorted.reshape(count, 1), cache)
+
+
+def fresh_attention(tables, q_sorted, o_sorted, rs_sorted, state, kv_sorted):
+    group, count, size = q_sorted.shape
+    tiles = count // TILE
+    body = functools.partial(_fresh_body, scale=size ** (-0.5))
+    column = pl.BlockSpec((TILE, 1), lambda t, tb: (t, 0))
+    lane = pl.BlockSpec((group * TILE, 1), lambda t, tb: (t, 0))
+    spec = pltpu.PrefetchScalarGridSpec(
+        num_scalar_prefetch=1,
+        grid=(tiles,),
+        in_specs=[
+            pl.BlockSpec((group, TILE, size), lambda t, tb: (0, t, 0)),
+            column,
+            column,
+            lane,
+            lane,
+            pl.BlockSpec((group * TILE, size), lambda t, tb: (t, 0)),
             pl.BlockSpec(kv_sorted.shape, lambda t, tb: (0, 0)),
-            pl.BlockSpec(cache.shape, lambda t, tb: (0, 0, 0)),
         ],
         out_specs=pl.BlockSpec((group, TILE, size), lambda t, tb: (0, t, 0)),
     )
@@ -122,8 +165,7 @@
         grid_spec=spec,
         out_shape=jax.ShapeDtypeStruct(q_sorted.shape, jnp.bfloat16),
         compiler_params=pltpu.CompilerParams(dimension_semantics=("arbitrary",)),
-        interpret=interpret,
-    )(tables, q_sorted, col(o_sorted), col(rs_sorted), col(req_sorted), kv_sorted, cache)
+    )(tables, q_sorted, o_sorted.reshape(count, 1), rs_sorted.reshape(count, 1), *state, kv_sorted)
 
 
 def rotate_columns(value, shift):
@@ -174,8 +216,7 @@
         jnp.where(destination[None, :] == slot_labels[:, None], slot_labels[None, :], 0), axis=1
     )
     arranged = jnp.take(key_value_cache, inverse, axis=1)
-    decode_cache = lax.all_to_all(arranged, "seq", split_axis=1, concat_axis=2, tiled=True)
-    full, decode_cache = lax.optimization_barrier((gather_heads(tokens), decode_cache))
+    full, arranged = lax.optimization_barrier((gather_heads(tokens), arranged))
     rows = full.shape[0]
     wide = full.astype(jnp.float32)
     normed = (wide * lax.rsqrt(jnp.mean(wide * wide, axis=1, keepdims=True) + epsilon)).astype(
@@ -222,17 +263,18 @@
     rs_sorted = jnp.take(my_order - position, perm)
     req_sorted = jnp.take(request, perm)
     q_sorted = jnp.take(query_rows, perm, axis=0)
+    tables = attention_tables(o_sorted, rs_sorted, req_sorted)
+    q_sorted, arranged = lax.optimization_barrier((q_sorted, arranged))
+    decode_cache = lax.all_to_all(arranged, "seq", split_axis=1, concat_axis=2, tiled=True)
     outs = []
     for head in range(local_heads):
-        result = sparse_attention(
-            q_sorted[:, head].transpose(1, 0, 2),
-            o_sorted,
-            rs_sorted,
-            req_sorted,
-            kv_sorted[:, head * 2 * HEAD_SIZE:(head + 1) * 2 * HEAD_SIZE],
-            cache[:, :, head * 2 * HEAD_SIZE:(head + 1) * 2 * HEAD_SIZE],
-        )
-        outs.append(jnp.take(result, unsort, axis=1).transpose(1, 0, 2))
+        q_head = q_sorted[:, head].transpose(1, 0, 2)
+        part = slice(head * 2 * HEAD_SIZE, (head + 1) * 2 * HEAD_SIZE)
+        state = cache_attention(tables, q_head, req_sorted, cache[:, :, part])
+        result = fresh_attention(tables, q_head, o_sorted, rs_sorted, state, kv_sorted[:, part])
+        outs.append(result)
+    outs, decode_cache = lax.optimization_barrier((outs, decode_cache))
+    outs = [jnp.take(result, unsort, axis=1).transpose(1, 0, 2) for result in outs]
     attn = jnp.stack(outs, axis=1).reshape(rows, local_heads * head_group * HEAD_SIZE)
     partial_value = jnp.dot(attn, w_out, preferred_element_type=jnp.float32)
     attn_out = scatter_heads(partial_value)

time: 268 us -> 268 us (level)
  waiting for transfers between devices: 66 us -> 59.9 us
  Pallas kernels: 32.7 us -> 37.7 us
    ppermute x7, waiting for transfers between devices: 29.1 us -> 10.2 us  [gather_heads(): got[shift] = lax.ppermute(piece, 'heads', pairs)]
    all_to_all x1, waiting for transfers between devices: 0.01 us -> 14.9 us  [on_device(): lax.all_to_all(arranged, 'seq', split_axis=1, concat_axis=2, tiled=True)]
    pallas_call x1 -> x2, Pallas kernels: 32.7 us -> 37.7 us  [the longest x1 19.1 us: fresh_attention(): pl.pallas_call(body, grid_spec=spec, out_shape=jax.ShapeDtypeStruct(q_sor...]
    unnamed x34 -> x32, local copies, waits for them, and re-layouts: 12.5 us -> 12.4 us
  transfers between devices with their start and end apart: 17 -> 17, of which waited for: 5 -> 7; matrix products, arithmetic and copies ran while one was open for 30% -> 29% of each run, Pallas kernels for 0% -> 0%
where the time goes in v1:
time: 268 us; the launch traced here: 265 us
  local copies, waits for them, and re-layouts  60.9 us (23%)
  waiting for transfers between devices  59.9 us (22%)
  starting transfers between devices  55.5 us (21%)
  Pallas kernels  37.7 us (14%)
  other arithmetic  22.9 us (9%)
  between operations  14.6 us (5%)
  matrix products  14 us (5%)
    ppermute x7, starting transfers between devices, scatter_heads(): total = total + lax.ppermute(piece, 'heads', pairs).astype(jnp.float32)  34.8 us
    pallas_call x1, Pallas kernels, fresh_attention(): pl.pallas_call(body, grid_spec=spec, out_shape=jax.ShapeDtypeStruct(q_sor...  19.1 us
    pallas_call x1, Pallas kernels, cache_attention(): pl.pallas_call(body, grid_spec=spec, out_shape=[jax.ShapeDtypeStruct((gro...  18.6 us
    all_gather x1, waiting for transfers between devices, on_device(): cache = lax.all_gather(used, 'seq', axis=1, tiled=True)  18 us
    gather x1, local copies, waits for them, and re-layouts, on_device(): kv_sorted = jnp.take(gathered, jnp.argsort(order), axis=0)  17 us
    ppermute x7, waiting for transfers between devices, scatter_heads(): total = total + lax.ppermute(piece, 'heads', pairs).astype(jnp.float32)  16.7 us
    ppermute x7, starting transfers between devices, gather_heads(): got[shift] = lax.ppermute(piece, 'heads', pairs)  15.5 us
    all_to_all x1, waiting for transfers between devices, on_device(): lax.all_to_all(arranged, 'seq', split_axis=1, concat_axis=2, tiled=True)  14.9 us
  transfers between devices with their start and end apart: 17, of which 7 were waited for; matrix products, arithmetic and copies ran while one was open for 29% of the time, Pallas kernels for 0%

profile of v1, /device:TPU:0, one launch (start us, length us, event | category | flops | bytes accessed | tf_op | source)
XLA Modules:
  0.0 265.3 jit_solution(13904110079721263440)
XLA Ops:
  7.2 6.5 %collective-permute-start = (bf16[256,640]{1,0:T(8,128)(2,1)}, bf16[256,640]{1,0:T(8,128)(2,1)}, u32[]{:S(2)}, u32[]{:S(2)}) collective-permute-start(bf16[256,640]{1,0:T(8,128)(2,1)} %param.12), channel_id=1, source_target_pairs={{0,7},{1,0},{2,1},{3,2},{4,3},{5,4},{6,5},{7,6},{8,15},{9,8},{10,9... | collective-permute-start | bytes 983048 | tf_op jit(solution)/shard_map/ppermute | solution.py:182
  14.4 3.9 %collective-permute-start.3 = (bf16[256,640]{1,0:T(8,128)(2,1)}, bf16[256,640]{1,0:T(8,128)(2,1)}, u32[]{:S(2)}, u32[]{:S(2)}) collective-permute-start(bf16[256,640]{1,0:T(8,128)(2,1)} %param.12), channel_id=1, source_target_pairs={{0,4},{1,5},{2,6},{3,7},{4,0},{5,1},{6,2},{7,3},{8,12},{9,13},{10,... | collective-permute-start | bytes 983048 | tf_op jit(solution)/shard_map/ppermute | solution.py:182
  20.6 7.0 %gather_fusion.4 = bf16[32,4,32,2,128]{4,3,2,1,0:T(2,128)(2,1)S(1)} fusion(bf16[4,32,32,2,128]{4,3,2,1,0:T(2,128)(2,1)} %param.21, s32[1024]{0:T(1024)S(1)} %pad_clamp_fusion.3), kind=kCustom, calls=%fused_computation.7 | custom fusion | bytes 4194432 | tf_op jit(solution)/shard_map/jit(_take)/gather | solution.py:218
  27.7 3.2 %fusion.3 = bf16[4,32,32,2,128]{4,3,2,0,1:T(2,128)(2,1)} fusion(bf16[32,4,32,2,128]{4,3,2,1,0:T(2,128)(2,1)S(1)} %gather_fusion.4, pred[32]{0:T(512)(128)(4,1)S(1)} %compare_and_fusion.3), kind=kLoop, calls=%fused_computation.21 | loop fusion | flops 1048576 | bytes 4194336 | tf_op jit(solution)/shard_map/jit(_take)/select_n | solution.py:218
  32.3 3.5 %collective-permute-start.5 = (bf16[256,640]{1,0:T(8,128)(2,1)}, bf16[256,640]{1,0:T(8,128)(2,1)S(1)}, u32[]{:S(2)}, u32[]{:S(2)}) collective-permute-start(bf16[256,640]{1,0:T(8,128)(2,1)} %param.12), channel_id=1, source_target_pairs={{0,2},{1,3},{2,4},{3,5},{4,6},{5,7},{6,0},{7,1},{8,10},{9,11},{10,... | collective-permute-start | bytes 983048 | tf_op jit(solution)/shard_map/ppermute | solution.py:182
  40.9 4.0 %collective-permute-done.4 = bf16[256,640]{1,0:T(8,128)(2,1)} collective-permute-done((bf16[256,640]{1,0:T(8,128)(2,1)}, bf16[256,640]{1,0:T(8,128)(2,1)}, u32[]{:S(2)}, u32[]{:S(2)}) %collective-permute-start.4) | collective-permute-done | bytes 327712 | tf_op jit(solution)/shard_map/ppermute | solution.py:182
  46.0 1.5 collective-permute-done.5
  47.6 4.7 %collective-permute-done.6 = bf16[256,640]{1,0:T(8,128)(2,1)S(1)} collective-permute-done((bf16[256,640]{1,0:T(8,128)(2,1)}, bf16[256,640]{1,0:T(8,128)(2,1)S(1)}, u32[]{:S(2)}, u32[]{:S(2)}) %collective-permute-start.6) | collective-permute-done | bytes 327712 | tf_op jit(solution)/shard_map/ppermute | solution.py:182
  62.4 1.5 slice_bitcast_fusion
  66.7 1.9 gather_fusion.9
  69.3 6.5 %fusion.22 = f32[256,640]{0,1:T(8,128)S(1)} fusion(bf16[5120,640]{1,0:T(8,128)(2,1)} %param.17, bf16[256,5120]{1,0:T(8,128)(2,1)} %copy-done.2, f32[256]{0:T(256)S(1)} %add_rsqrt_fusion), kind=kOutput, calls=%fused_computation.121 | convolution fusion | flops 1681653760 | bytes 9831424 | tf_op jit(solution)/shard_map/dot_general | solution.py:227
  79.0 4.9 %all-to-all-start = ((bf16[4,32,32,2,128]{4,3,2,0,1:T(2,128)(2,1)}), bf16[4,32,32,2,128]{4,3,2,0,1:T(2,128)(2,1)S(1)}, u32[]{:S(2)}, u32[]{:S(2)}) async-start(bf16[4,32,32,2,128]{4,3,2,0,1:T(2,128)(2,1)} %fusion.3), calls=%async_computation | async-start | bytes 4194304 | tf_op jit(solution)/shard_map/all_to_all | solution.py:268
  83.9 1.9 gather_fusion.10
  85.8 1.9 gather_fusion.11
  87.8 5.8 %sort.17 = (s32[4096]{0:T(1024)}, s32[4096]{0:T(1024)S(1)}) sort(s32[4096]{0:T(1024)S(1)} %copy-done.4, s32[4096]{0:T(1024)S(1)} %iota.43), dimensions={0}, to_apply=%region_7.9 | sort | flops 49152 | bytes 65536 | tf_op jit(solution)/shard_map/jit(argsort)/sort | solution.py:251
  99.2 14.9 %all-to-all-done = bf16[4,32,32,2,128]{4,3,2,0,1:T(2,128)(2,1)S(1)} async-done(((bf16[4,32,32,2,128]{4,3,2,0,1:T(2,128)(2,1)}), bf16[4,32,32,2,128]{4,3,2,0,1:T(2,128)(2,1)S(1)}, u32[]{:S(2)}, u32[]{:S(2)}) %all-to-all-start) | async-done | bytes 2097184 | tf_op jit(solution)/shard_map/all_to_all | solution.py:268
  114.1 3.3 %copy.39 = bf16[4,16,2,32,2,128]{5,4,3,1,2,0:T(2,128)(2,1)} copy(bf16[4,16,2,32,2,128]{5,4,3,0,2,1:T(2,128)(2,1)S(1)} %bitcast.72) | data formatting | bytes 4194304 | tf_op jit(solution)/shard_map/all_to_all | solution.py:268
  117.4 3.3 %copy.36 = bf16[4096,256]{1,0:T(8,128)(2,1)S(1)} copy(bf16[4096,256]{0,1:T(8,128)(2,1)} %bitcast.75) | data formatting | bytes 4194304 | tf_op jit(solution)/shard_map/all_gather | solution.py:250
  120.7 17.0 %gather_fusion.7 = bf16[4096,256]{1,0:T(8,128)(2,1)} fusion(bf16[4096,256]{1,0:T(8,128)(2,1)S(1)} %copy.36, s32[4096]{0:T(1024)S(1)} %fusion.15), kind=kCustom, calls=%fused_computation.10 | custom fusion | bytes 4210688 | tf_op jit(solution)/shard_map/jit(_take)/gather | solution.py:251
  137.7 3.0 %broadcast_select_fusion.1.kv_ref = bf16[4096,256]{1,0:T(8,128)(2,1)} fusion(bf16[4096,256]{1,0:T(8,128)(2,1)} %gather_fusion.7, pred[4096]{0:T(1024)(128)(4,1)S(1)} %compare_and_fusion), kind=kLoop, calls=%fused_computation.22 | loop fusion | flops 1048576 | bytes 4198400 | tf_op jit(solution)/shard_map/jit(_take)/select_n | solution.py:251
  140.7 18.0 %all-gather.4.cloned.1.call-done.cache_ref = bf16[24,512,256]{2,1,0:T(8,128)(2,1)} async-done(((bf16[24,32,256]{2,1,0:T(8,128)(2,1)}), bf16[24,512,256]{2,1,0:T(8,128)(2,1)}) %all-gather.4.cloned.1.call-update) | async-done | bytes 6291472 | tf_op jit(solution)/shard_map/all_gather | solution.py:257
  158.7 18.6 %shard_map.113 = (f32[1280,1]{1,0:T(8,128)}, f32[1280,1]{1,0:T(8,128)}, f32[1280,128]{1,0:T(8,128)}) custom-call(s32[4,8]{1,0:T(4,128)} %pad_add_fusion.tables, bf16[5,256,128]{2,1,0:T(8,128)(2,1)} %bitcast.73, s32[256,1]{1,0:T(8,128)} %copy.35.req_ref, bf16[24,512,256]{2,1,0:T(8,128)(2,1)} %all-gather.4.cloned.1.call-done.cache_ref), custom_call_target="tpu_custom_call" | custom-call | tf_op jit(solution)/shard_map/pallas_call | solution.py:131
  177.3 19.1 %shard_map.114 = bf16[5,256,128]{2,1,0:T(8,128)(2,1)} custom-call(s32[4,8]{1,0:T(4,128)} %pad_add_fusion.tables, bf16[5,256,128]{2,1,0:T(8,128)(2,1)} %bitcast.74, s32[256,1]{1,0:T(8,128)} %copy.37.o_ref, s32[256,1]{1,0:T(8,128)} %copy.38.rs_ref, f32[1280,1]{1,0:T(8,128)} %get-tuple-element.16.top_ref, f32[1280,1]{1,0:T(8,128)} %get-tuple-element.17.total_ref, ...), custom_call_target="tpu_custom_call" | custom-call | tf_op jit(solution)/shard_map/pallas_call | solution.py:163
  199.0 5.2 %convolution_convert_fusion = bf16[256,5120]{1,0:T(8,128)(2,1)S(1)} fusion(bf16[256,640]{0,1:T(8,128)(2,1)S(1)} %bitcast.77, bf16[640,5120]{1,0:T(8,128)(2,1)} %param.20), kind=kOutput, calls=%fused_computation.14 | convolution fusion | flops 1679032320 | bytes 9502720 | tf_op jit(solution)/shard_map/dot_general | solution.py:279
  205.9 2.9 %collective-permute-start.10 = (bf16[256,640]{1,0:T(8,128)(2,1)S(1)}, bf16[256,640]{1,0:T(8,128)(2,1)S(1)}, u32[]{:S(2)}, u32[]{:S(2)}) collective-permute-start(bf16[256,640]{1,0:T(8,128)(2,1)S(1)} %get-tuple-element.28), channel_id=1, source_target_pairs={{0,4},{1,5},{2,6},{3,7},{4,0},{5,1},{6,2},{7,3},{8,12},{9,13},{10,... | collective-permute-start | bytes 983048 | tf_op jit(solution)/shard_map/ppermute | solution.py:197
  208.8 1.6 collective-permute-start.11
  210.4 5.0 %collective-permute-start.12 = (bf16[256,640]{1,0:T(8,128)(2,1)S(1)}, bf16[256,640]{1,0:T(8,128)(2,1)S(1)}, u32[]{:S(2)}, u32[]{:S(2)}) collective-permute-start(bf16[256,640]{1,0:T(8,128)(2,1)S(1)} %get-tuple-element.26), channel_id=1, source_target_pairs={{0,6},{1,7},{2,0},{3,1},{4,2},{5,3},{6,4},{7,5},{8,14},{9,15},{10,... | collective-permute-start | bytes 983048 | tf_op jit(solution)/shard_map/ppermute | solution.py:197
  215.4 1.4 collective-permute-start.13
  217.4 16.5 %collective-permute-start.8 = (bf16[256,640]{1,0:T(8,128)(2,1)S(1)}, bf16[256,640]{1,0:T(8,128)(2,1)S(1)}, u32[]{:S(2)}, u32[]{:S(2)}) collective-permute-start(bf16[256,640]{1,0:T(8,128)(2,1)S(1)} %get-tuple-element.30), channel_id=1, source_target_pairs={{0,2},{1,3},{2,4},{3,5},{4,6},{5,7},{6,0},{7,1},{8,10},{9,11},{10,... | collective-permute-start | bytes 983048 | tf_op jit(solution)/shard_map/ppermute | solution.py:197
  233.9 6.8 %collective-permute-start.9 = (bf16[256,640]{1,0:T(8,128)(2,1)S(1)}, bf16[256,640]{1,0:T(8,128)(2,1)S(1)}, u32[]{:S(2)}, u32[]{:S(2)}) collective-permute-start(bf16[256,640]{1,0:T(8,128)(2,1)S(1)} %get-tuple-element.29), channel_id=1, source_target_pairs={{0,3},{1,4},{2,5},{3,6},{4,7},{5,0},{6,1},{7,2},{8,11},{9,12},{10,... | collective-permute-start | bytes 983048 | tf_op jit(solution)/shard_map/ppermute | solution.py:197
  240.7 8.6 %collective-permute-done.8 = bf16[256,640]{1,0:T(8,128)(2,1)S(1)} collective-permute-done((bf16[256,640]{1,0:T(8,128)(2,1)S(1)}, bf16[256,640]{1,0:T(8,128)(2,1)S(1)}, u32[]{:S(2)}, u32[]{:S(2)}) %collective-permute-start.8) | collective-permute-done | bytes 327712 | tf_op jit(solution)/shard_map/ppermute | solution.py:197
  249.3 8.1 %collective-permute-done.9 = bf16[256,640]{1,0:T(8,128)(2,1)S(1)} collective-permute-done((bf16[256,640]{1,0:T(8,128)(2,1)S(1)}, bf16[256,640]{1,0:T(8,128)(2,1)S(1)}, u32[]{:S(2)}, u32[]{:S(2)}) %collective-permute-start.9) | collective-permute-done | bytes 327712 | tf_op jit(solution)/shard_map/ppermute | solution.py:197
  (117 shorter events, 38.6 us)
Async XLA Ops:
  7.2 51.4 %copy-start = (bf16[5120,128]{1,0:T(8,128)(2,1)S(1)}, bf16[5120,128]{1,0:T(8,128)(2,1)}, u32[]{:S(2)}) copy-start(bf16[5120,128]{1,0:T(8,128)(2,1)} %param.18) | copy-start | bytes 3932164
  7.2 23.7 %copy-start.4 = (s32[4096]{0:T(1024)S(1)}, s32[4096]{0:T(1024)}, u32[]{:S(2)}) copy-start(s32[4096]{0:T(1024)} %param.13) | copy-start | bytes 49156
  7.2 110.2 %all-gather.6.cloned.1.call-start = ((), (), s32[]{:S(2)}) async-start(), calls=%async_computation.2 | async-start | bytes 2228224 | tf_op jit(solution)/shard_map/all_gather | solution.py:250
  7.2 25.0 %collective-permute-start = (bf16[256,640]{1,0:T(8,128)(2,1)}, bf16[256,640]{1,0:T(8,128)(2,1)}, u32[]{:S(2)}, u32[]{:S(2)}) collective-permute-start(bf16[256,640]{1,0:T(8,128)(2,1)} %param.12), channel_id=1, source_target_pairs={{0,7},{1,0},{2,1},{3,2},{4,3},{5,4},{6,5},{7,6},{8,15},{9,8},{10,9... | collective-permute-start | bytes 983048 | tf_op jit(solution)/shard_map/ppermute | solution.py:182
  13.7 23.0 %collective-permute-start.1 = (bf16[256,640]{1,0:T(8,128)(2,1)}, bf16[256,640]{1,0:T(8,128)(2,1)}, u32[]{:S(2)}, u32[]{:S(2)}) collective-permute-start(bf16[256,640]{1,0:T(8,128)(2,1)} %param.12), channel_id=1, source_target_pairs={{0,6},{1,7},{2,0},{3,1},{4,2},{5,3},{6,4},{7,5},{8,14},{9,15},{10,... | collective-permute-start | bytes 983048 | tf_op jit(solution)/shard_map/ppermute | solution.py:182
  14.4 24.5 %collective-permute-start.2 = (bf16[256,640]{1,0:T(8,128)(2,1)}, bf16[256,640]{1,0:T(8,128)(2,1)}, u32[]{:S(2)}, u32[]{:S(2)}) collective-permute-start(bf16[256,640]{1,0:T(8,128)(2,1)} %param.12), channel_id=1, source_target_pairs={{0,5},{1,6},{2,7},{3,0},{4,1},{5,2},{6,3},{7,4},{8,13},{9,14},{10,... | collective-permute-start | bytes 983048 | tf_op jit(solution)/shard_map/ppermute | solution.py:182
  14.4 25.5 %collective-permute-start.3 = (bf16[256,640]{1,0:T(8,128)(2,1)}, bf16[256,640]{1,0:T(8,128)(2,1)}, u32[]{:S(2)}, u32[]{:S(2)}) collective-permute-start(bf16[256,640]{1,0:T(8,128)(2,1)} %param.12), channel_id=1, source_target_pairs={{0,4},{1,5},{2,6},{3,7},{4,0},{5,1},{6,2},{7,3},{8,12},{9,13},{10,... | collective-permute-start | bytes 983048 | tf_op jit(solution)/shard_map/ppermute | solution.py:182
  18.3 26.7 %collective-permute-start.4 = (bf16[256,640]{1,0:T(8,128)(2,1)}, bf16[256,640]{1,0:T(8,128)(2,1)}, u32[]{:S(2)}, u32[]{:S(2)}) collective-permute-start(bf16[256,640]{1,0:T(8,128)(2,1)} %param.12), channel_id=1, source_target_pairs={{0,3},{1,4},{2,5},{3,6},{4,7},{5,0},{6,1},{7,2},{8,11},{9,12},{10,... | collective-permute-start | bytes 983048 | tf_op jit(solution)/shard_map/ppermute | solution.py:182
  30.9 21.4 %copy-start.3 = (bf16[256,640]{1,0:T(8,128)(2,1)S(1)}, bf16[256,640]{1,0:T(8,128)(2,1)}, u32[]{:S(2)}) copy-start(bf16[256,640]{1,0:T(8,128)(2,1)} %param.12) | copy-start | bytes 983044
  32.3 15.2 %collective-permute-start.5 = (bf16[256,640]{1,0:T(8,128)(2,1)}, bf16[256,640]{1,0:T(8,128)(2,1)S(1)}, u32[]{:S(2)}, u32[]{:S(2)}) collective-permute-start(bf16[256,640]{1,0:T(8,128)(2,1)} %param.12), channel_id=1, source_target_pairs={{0,2},{1,3},{2,4},{3,5},{4,6},{5,7},{6,0},{7,1},{8,10},{9,11},{10,... | collective-permute-start | bytes 983048 | tf_op jit(solution)/shard_map/ppermute | solution.py:182
  36.8 15.5 %collective-permute-start.6 = (bf16[256,640]{1,0:T(8,128)(2,1)}, bf16[256,640]{1,0:T(8,128)(2,1)S(1)}, u32[]{:S(2)}, u32[]{:S(2)}) collective-permute-start(bf16[256,640]{1,0:T(8,128)(2,1)} %param.12), channel_id=1, source_target_pairs={{0,1},{1,2},{2,3},{3,4},{4,5},{5,6},{6,7},{7,0},{8,9},{9,10},{10,1... | collective-permute-start | bytes 983048 | tf_op jit(solution)/shard_map/ppermute | solution.py:182
  57.7 2.0 copy-start.6
  57.9 2.9 %copy-start.2 = (bf16[256,5120]{1,0:T(8,128)(2,1)}, bf16[256,5120]{1,0:T(8,128)(2,1)S(1)}, u32[]{:S(2)}) copy-start(bf16[256,5120]{1,0:T(8,128)(2,1)S(1)} %constant_dynamic-slice_fusion) | copy-start | bytes 7864324
  58.5 3.6 %copy-start.5 = (s32[12,2]{0,1:T(2,128)S(1)}, s32[12,2]{0,1:T(2,128)}, u32[]{:S(2)}) copy-start(s32[12,2]{0,1:T(2,128)} %param.15) | copy-start | bytes 292
  61.9 96.8 %all-gather.4.cloned.1.call-start = ((), (), s32[]{:S(2)}) async-start(), calls=%async_computation.1 | async-start | bytes 6684672 | tf_op jit(solution)/shard_map/all_gather | solution.py:257
  79.0 35.1 %all-to-all-start = ((bf16[4,32,32,2,128]{4,3,2,0,1:T(2,128)(2,1)}), bf16[4,32,32,2,128]{4,3,2,0,1:T(2,128)(2,1)S(1)}, u32[]{:S(2)}, u32[]{:S(2)}) async-start(bf16[4,32,32,2,128]{4,3,2,0,1:T(2,128)(2,1)} %fusion.3), calls=%async_computation | async-start | bytes 4194304 | tf_op jit(solution)/shard_map/all_to_all | solution.py:268
  199.0 59.5 %copy-start.1 = (bf16[5120,128]{1,0:T(8,128)(2,1)S(1)}, bf16[5120,128]{1,0:T(8,128)(2,1)}, u32[]{:S(2)}) copy-start(bf16[5120,128]{1,0:T(8,128)(2,1)} %param.18) | copy-start | bytes 3932164
  205.9 11.6 %collective-permute-start.10 = (bf16[256,640]{1,0:T(8,128)(2,1)S(1)}, bf16[256,640]{1,0:T(8,128)(2,1)S(1)}, u32[]{:S(2)}, u32[]{:S(2)}) collective-permute-start(bf16[256,640]{1,0:T(8,128)(2,1)S(1)} %get-tuple-element.28), channel_id=1, source_target_pairs={{0,4},{1,5},{2,6},{3,7},{4,0},{5,1},{6,2},{7,3},{8,12},{9,13},{10,... | collective-permute-start | bytes 983048 | tf_op jit(solution)/shard_map/ppermute | solution.py:197
  208.8 25.1 %collective-permute-start.11 = (bf16[256,640]{1,0:T(8,128)(2,1)S(1)}, bf16[256,640]{1,0:T(8,128)(2,1)S(1)}, u32[]{:S(2)}, u32[]{:S(2)}) collective-permute-start(bf16[256,640]{1,0:T(8,128)(2,1)S(1)} %get-tuple-element.27), channel_id=1, source_target_pairs={{0,5},{1,6},{2,7},{3,0},{4,1},{5,2},{6,3},{7,4},{8,13},{9,14},{10,... | collective-permute-start | bytes 983048 | tf_op jit(solution)/shard_map/ppermute | solution.py:197
  210.4 30.3 %collective-permute-start.12 = (bf16[256,640]{1,0:T(8,128)(2,1)S(1)}, bf16[256,640]{1,0:T(8,128)(2,1)S(1)}, u32[]{:S(2)}, u32[]{:S(2)}) collective-permute-start(bf16[256,640]{1,0:T(8,128)(2,1)S(1)} %get-tuple-element.26), channel_id=1, source_target_pairs={{0,6},{1,7},{2,0},{3,1},{4,2},{5,3},{6,4},{7,5},{8,14},{9,15},{10,... | collective-permute-start | bytes 983048 | tf_op jit(solution)/shard_map/ppermute | solution.py:197
  215.4 25.3 %collective-permute-start.13 = (bf16[256,640]{1,0:T(8,128)(2,1)S(1)}, bf16[256,640]{1,0:T(8,128)(2,1)S(1)}, u32[]{:S(2)}, u32[]{:S(2)}) collective-permute-start(bf16[256,640]{1,0:T(8,128)(2,1)S(1)} %get-tuple-element.31), channel_id=1, source_target_pairs={{0,7},{1,0},{2,1},{3,2},{4,3},{5,4},{6,5},{7,6},{8,15},{9,8},{10,9... | collective-permute-start | bytes 983048 | tf_op jit(solution)/shard_map/ppermute | solution.py:197
  216.9 23.8 %collective-permute-start.7 = (bf16[256,640]{1,0:T(8,128)(2,1)S(1)}, bf16[256,640]{1,0:T(8,128)(2,1)S(1)}, u32[]{:S(2)}, u32[]{:S(2)}) collective-permute-start(bf16[256,640]{1,0:T(8,128)(2,1)S(1)} %get-tuple-element.25), channel_id=1, source_target_pairs={{0,1},{1,2},{2,3},{3,4},{4,5},{5,6},{6,7},{7,0},{8,9},{9,10},{10,1... | collective-permute-start | bytes 983048 | tf_op jit(solution)/shard_map/ppermute | solution.py:197
  217.4 31.8 %collective-permute-start.8 = (bf16[256,640]{1,0:T(8,128)(2,1)S(1)}, bf16[256,640]{1,0:T(8,128)(2,1)S(1)}, u32[]{:S(2)}, u32[]{:S(2)}) collective-permute-start(bf16[256,640]{1,0:T(8,128)(2,1)S(1)} %get-tuple-element.30), channel_id=1, source_target_pairs={{0,2},{1,3},{2,4},{3,5},{4,6},{5,7},{6,0},{7,1},{8,10},{9,11},{10,... | collective-permute-start | bytes 983048 | tf_op jit(solution)/shard_map/ppermute | solution.py:197
  233.9 23.5 %collective-permute-start.9 = (bf16[256,640]{1,0:T(8,128)(2,1)S(1)}, bf16[256,640]{1,0:T(8,128)(2,1)S(1)}, u32[]{:S(2)}, u32[]{:S(2)}) collective-permute-start(bf16[256,640]{1,0:T(8,128)(2,1)S(1)} %get-tuple-element.29), channel_id=1, source_target_pairs={{0,3},{1,4},{2,5},{3,6},{4,7},{5,0},{6,1},{7,2},{8,11},{9,12},{10,... | collective-permute-start | bytes 983048 | tf_op jit(solution)/shard_map/ppermute | solution.py:197
Sparse Core Ops, SparseCore 0:
  62.0 46.9 all-gather.5
  110.7 47.9 all-gather.3

commit v2 on v1

--- a/solution.py
+++ b/solution.py
@@ -210,13 +210,21 @@
     w_out,
     key_value_cache,
 ):
+    local_heads = key_weight.shape[1] // HEAD_SIZE
     slots = destination.shape[0]
     slot_labels = jnp.arange(slots, dtype=jnp.int32)
     inverse = jnp.sum(
         jnp.where(destination[None, :] == slot_labels[:, None], slot_labels[None, :], 0), axis=1
     )
     arranged = jnp.take(key_value_cache, inverse, axis=1)
-    full, arranged = lax.optimization_barrier((gather_heads(tokens), arranged))
+    layer_zero = key_value_cache[0]
+    used = jnp.take(layer_zero, block_table.reshape(-1), axis=0)
+    pool, span = used.shape[0], used.shape[1]
+    used = used.reshape(pool, span, 2, local_heads, HEAD_SIZE).transpose(0, 1, 3, 2, 4)
+    used = used.reshape(pool, span, local_heads * 2 * HEAD_SIZE)
+    cache = lax.all_gather(used, "seq", axis=1, tiled=True)
+    by_order = jnp.argsort(order)
+    full, arranged, cache, by_order = lax.optimization_barrier((gather_heads(tokens), arranged, cache, by_order))
     rows = full.shape[0]
     wide = full.astype(jnp.float32)
     normed = (wide * lax.rsqrt(jnp.mean(wide * wide, axis=1, keepdims=True) + epsilon)).astype(
@@ -248,13 +256,7 @@
         axis=2,
     ).reshape(rows, local_heads * 2 * HEAD_SIZE)
     gathered = lax.all_gather(fresh_rows, "seq", axis=0, tiled=True)
-    kv_sorted = jnp.take(gathered, jnp.argsort(order), axis=0)
-    layer_zero = key_value_cache[0]
-    used = jnp.take(layer_zero, block_table.reshape(-1), axis=0)
-    pool, span = used.shape[0], used.shape[1]
-    used = used.reshape(pool, span, 2, local_heads, HEAD_SIZE).transpose(0, 1, 3, 2, 4)
-    used = used.reshape(pool, span, local_heads * 2 * HEAD_SIZE)
-    cache = lax.all_gather(used, "seq", axis=1, tiled=True)
+    kv_sorted = jnp.take(gathered, by_order, axis=0)
     earlier = (my_order[None, :] < my_order[:, None]).astype(jnp.int32)
     unsort = jnp.sum(earlier, axis=1)
     slots_of = jnp.arange(rows, dtype=jnp.int32)
@@ -264,8 +266,6 @@
     req_sorted = jnp.take(request, perm)
     q_sorted = jnp.take(query_rows, perm, axis=0)
     tables = attention_tables(o_sorted, rs_sorted, req_sorted)
-    q_sorted, arranged = lax.optimization_barrier((q_sorted, arranged))
-    decode_cache = lax.all_to_all(arranged, "seq", split_axis=1, concat_axis=2, tiled=True)
     outs = []
     for head in range(local_heads):
         q_head = q_sorted[:, head].transpose(1, 0, 2)
@@ -273,10 +273,11 @@
         state = cache_attention(tables, q_head, req_sorted, cache[:, :, part])
         result = fresh_attention(tables, q_head, o_sorted, rs_sorted, state, kv_sorted[:, part])
         outs.append(result)
-    outs, decode_cache = lax.optimization_barrier((outs, decode_cache))
     outs = [jnp.take(result, unsort, axis=1).transpose(1, 0, 2) for result in outs]
     attn = jnp.stack(outs, axis=1).reshape(rows, local_heads * head_group * HEAD_SIZE)
     partial_value = jnp.dot(attn, w_out, preferred_element_type=jnp.float32)
+    partial_value, arranged = lax.optimization_barrier((partial_value, arranged))
+    decode_cache = lax.all_to_all(arranged, "seq", split_axis=1, concat_axis=2, tiled=True)
     attn_out = scatter_heads(partial_value)
     return (attn_out, decode_cache)
 

time: 268 us -> 256 us (0.955); the launches traced: 265 us -> 257 us
  starting transfers between devices: 55.5 us -> 38.4 us
  local copies, waits for them, and re-layouts: 60.9 us -> 64.7 us
  matrix products: 14 us -> 17.1 us
  waiting for transfers between devices: 59.9 us -> 57 us
    ppermute x7, waiting for transfers between devices: 16.7 us -> 38.4 us  [scatter_heads(): total = total + lax.ppermute(piece, 'heads', pairs).astype(jnp.float32)]
    ppermute x7, starting transfers between devices: 34.8 us -> 19.1 us  [scatter_heads(): total = total + lax.ppermute(piece, 'heads', pairs).astype(jnp.float32)]
    all_to_all x1, waiting for transfers between devices: 14.9 us -> 0.01 us  [on_device(): lax.all_to_all(arranged, 'seq', split_axis=1, concat_axis=2, tiled=True)]
    all_gather x1, waiting for transfers between devices: 18 us -> 7.28 us  [on_device(): cache = lax.all_gather(used, 'seq', axis=1, tiled=True)]
    unnamed x32 -> x34, local copies, waits for them, and re-layouts: 12.4 us -> 13.3 us
  transfers between devices with their start and end apart: 17 -> 17, of which waited for: 7 -> 7; matrix products, arithmetic and copies ran while one was open for 29% -> 22% of each run, Pallas kernels for 0% -> 7%
where the time goes in v2:
time: 256 us; the launch traced here: 257 us
  local copies, waits for them, and re-layouts  64.7 us (25%)
  waiting for transfers between devices  57 us (22%)
  Pallas kernels  40.3 us (16%)
  starting transfers between devices  38.4 us (15%)
  other arithmetic  24.5 us (10%)
  matrix products  17.1 us (7%)
  between operations  14.6 us (6%)
    ppermute x7, waiting for transfers between devices, scatter_heads(): total = total + lax.ppermute(piece, 'heads', pairs).astype(jnp.float32)  38.4 us
    pallas_call x1, Pallas kernels, fresh_attention(): pl.pallas_call(body, grid_spec=spec, out_shape=jax.ShapeDtypeStruct(q_sor...  21.4 us
    ppermute x7, starting transfers between devices, scatter_heads(): total = total + lax.ppermute(piece, 'heads', pairs).astype(jnp.float32)  19.1 us
    pallas_call x1, Pallas kernels, cache_attention(): pl.pallas_call(body, grid_spec=spec, out_shape=[jax.ShapeDtypeStruct((gro...  18.9 us
    gather x1, local copies, waits for them, and re-layouts, on_device(): kv_sorted = jnp.take(gathered, by_order, axis=0)  17 us
    ppermute x7, starting transfers between devices, gather_heads(): got[shift] = lax.ppermute(piece, 'heads', pairs)  14.7 us
    unnamed x34, local copies, waits for them, and re-layouts  13.3 us
    ppermute x7, waiting for transfers between devices, gather_heads(): got[shift] = lax.ppermute(piece, 'heads', pairs)  11 us
  transfers between devices with their start and end apart: 17, of which 7 were waited for; matrix products, arithmetic and copies ran while one was open for 22% of the time, Pallas kernels for 7%

profile of v2, /device:TPU:0, one launch (start us, length us, event | category | flops | bytes accessed | tf_op | source)
XLA Modules:
  0.0 256.5 jit_solution(15066009564365443105)
XLA Ops:
  8.3 1.5 slice_bitcast_fusion
  12.3 6.5 %collective-permute-start = (bf16[256,640]{1,0:T(8,128)(2,1)}, bf16[256,640]{1,0:T(8,128)(2,1)}, u32[]{:S(2)}, u32[]{:S(2)}) collective-permute-start(bf16[256,640]{1,0:T(8,128)(2,1)} %param.12), channel_id=1, source_target_pairs={{0,7},{1,0},{2,1},{3,2},{4,3},{5,4},{6,5},{7,6},{8,15},{9,8},{10,9... | collective-permute-start | bytes 983048 | tf_op jit(solution)/shard_map/ppermute | solution.py:182
  19.5 3.9 %collective-permute-start.3 = (bf16[256,640]{1,0:T(8,128)(2,1)}, bf16[256,640]{1,0:T(8,128)(2,1)}, u32[]{:S(2)}, u32[]{:S(2)}) collective-permute-start(bf16[256,640]{1,0:T(8,128)(2,1)} %param.12), channel_id=1, source_target_pairs={{0,4},{1,5},{2,6},{3,7},{4,0},{5,1},{6,2},{7,3},{8,12},{9,13},{10,... | collective-permute-start | bytes 983048 | tf_op jit(solution)/shard_map/ppermute | solution.py:182
  25.4 1.9 gather_fusion.11
  27.4 1.9 gather_fusion.9
  29.5 1.9 gather_fusion.10
  31.6 7.1 %gather_fusion.4 = bf16[32,4,32,2,128]{4,3,2,1,0:T(2,128)(2,1)S(1)} fusion(bf16[4,32,32,2,128]{4,3,2,1,0:T(2,128)(2,1)} %param.21, s32[1024]{0:T(1024)S(1)} %pad_clamp_fusion.3), kind=kCustom, calls=%fused_computation.7 | custom fusion | bytes 4194432 | tf_op jit(solution)/shard_map/jit(_take)/gather | solution.py:219
  38.7 5.8 %sort.17 = (s32[4096]{0:T(1024)}, s32[4096]{0:T(1024)S(1)}) sort(s32[4096]{0:T(1024)S(1)} %copy-done.4, s32[4096]{0:T(1024)S(1)} %iota.42), dimensions={0}, to_apply=%region_6.8 | sort | flops 49152 | bytes 65536 | tf_op jit(solution)/shard_map/jit(argsort)/sort | solution.py:226
  45.7 3.3 %fusion.3 = bf16[4,32,32,2,128]{4,3,2,0,1:T(2,128)(2,1)} fusion(bf16[32,4,32,2,128]{4,3,2,1,0:T(2,128)(2,1)S(1)} %gather_fusion.4, pred[32]{0:T(512)(128)(4,1)S(1)} %compare_and_fusion.3), kind=kLoop, calls=%fused_computation.20 | loop fusion | flops 1048576 | bytes 4194336 | tf_op jit(solution)/shard_map/jit(_take)/select_n | solution.py:219
  49.0 3.4 %collective-permute-start.5 = (bf16[256,640]{1,0:T(8,128)(2,1)}, bf16[256,640]{1,0:T(8,128)(2,1)S(1)}, u32[]{:S(2)}, u32[]{:S(2)}) collective-permute-start(bf16[256,640]{1,0:T(8,128)(2,1)} %param.12), channel_id=1, source_target_pairs={{0,2},{1,3},{2,4},{3,5},{4,6},{5,7},{6,0},{7,1},{8,10},{9,11},{10,... | collective-permute-start | bytes 983048 | tf_op jit(solution)/shard_map/ppermute | solution.py:182
  57.9 6.3 %collective-permute-done.5 = bf16[256,640]{1,0:T(8,128)(2,1)S(1)} collective-permute-done((bf16[256,640]{1,0:T(8,128)(2,1)}, bf16[256,640]{1,0:T(8,128)(2,1)S(1)}, u32[]{:S(2)}, u32[]{:S(2)}) %collective-permute-start.5) | collective-permute-done | bytes 327712 | tf_op jit(solution)/shard_map/ppermute | solution.py:182
  64.2 4.7 %collective-permute-done.6 = bf16[256,640]{1,0:T(8,128)(2,1)S(1)} collective-permute-done((bf16[256,640]{1,0:T(8,128)(2,1)S(1)}, bf16[256,640]{1,0:T(8,128)(2,1)S(1)}, u32[]{:S(2)}, u32[]{:S(2)}) %collective-permute-start.6) | collective-permute-done | bytes 327712 | tf_op jit(solution)/shard_map/ppermute | solution.py:182
  74.4 1.7 constant_dynamic-slice_fusion
  76.2 7.3 %all-gather.4.cloned.1.call-done.cache_ref = bf16[24,512,256]{2,1,0:T(8,128)(2,1)} async-done(((bf16[24,32,256]{2,1,0:T(8,128)(2,1)}), bf16[24,512,256]{2,1,0:T(8,128)(2,1)}) %all-gather.4.cloned.1.call-update) | async-done | bytes 6291472 | tf_op jit(solution)/shard_map/all_gather | solution.py:225
  83.4 2.5 fusion
  85.9 2.8 %fusion.4 = bf16[256,1,128]{0,2,1:T(8,128)(2,1)S(1)} fusion(bf16[5120,128]{1,0:T(8,128)(2,1)S(1)} %copy-done, bf16[256,5120]{1,0:T(8,128)(2,1)} %constant_dynamic-slice_fusion, f32[256]{0:T(256)S(1)} %add_rsqrt_fusion), kind=kOutput, calls=%fused_computation.24 | convolution fusion | flops 339509248 | bytes 3998720 | tf_op jit(solution)/shard_map/dot_general | solution.py:237
  97.2 6.5 %fusion.23 = f32[256,640]{0,1:T(8,128)S(1)} fusion(bf16[5120,640]{1,0:T(8,128)(2,1)} %param.17, bf16[256,5120]{1,0:T(8,128)(2,1)} %constant_dynamic-slice_fusion, f32[256]{0:T(256)S(1)} %add_rsqrt_fusion), kind=kOutput, calls=%fused_computation.121 | convolution fusion | flops 1681653760 | bytes 9831424 | tf_op jit(solution)/shard_map/dot_general | solution.py:235
  106.9 18.9 %shard_map.113 = (f32[1280,1]{1,0:T(8,128)}, f32[1280,1]{1,0:T(8,128)}, f32[1280,128]{1,0:T(8,128)}) custom-call(s32[4,8]{1,0:T(4,128)} %pad_add_fusion.tables, bf16[5,256,128]{2,1,0:T(8,128)(2,1)} %fusion.7.q_ref, s32[256,1]{1,0:T(8,128)} %copy.36.req_ref, bf16[24,512,256]{2,1,0:T(8,128)(2,1)} %all-gather.4.cloned.1.call-done.cache_ref), custom_call_target="tpu_custom_call" | custom-call | tf_op jit(solution)/shard_map/pallas_call | solution.py:131
  126.0 3.3 %copy.37 = bf16[4096,256]{1,0:T(8,128)(2,1)S(1)} copy(bf16[4096,256]{0,1:T(8,128)(2,1)} %bitcast.70) | data formatting | bytes 4194304 | tf_op jit(solution)/shard_map/all_gather | solution.py:258
  129.3 17.0 %gather_fusion.7 = bf16[4096,256]{1,0:T(8,128)(2,1)} fusion(bf16[4096,256]{1,0:T(8,128)(2,1)S(1)} %copy.37, s32[4096]{0:T(1024)S(1)} %fusion.16), kind=kCustom, calls=%fused_computation.10 | custom fusion | bytes 4210688 | tf_op jit(solution)/shard_map/jit(_take)/gather | solution.py:259
  146.3 2.9 %broadcast_select_fusion.1.kv_ref = bf16[4096,256]{1,0:T(8,128)(2,1)} fusion(bf16[4096,256]{1,0:T(8,128)(2,1)} %gather_fusion.7, pred[4096]{0:T(1024)(128)(4,1)S(1)} %compare_and_fusion), kind=kLoop, calls=%fused_computation.21 | loop fusion | flops 1048576 | bytes 4198400 | tf_op jit(solution)/shard_map/jit(_take)/select_n | solution.py:259
  149.2 21.4 %shard_map.114 = bf16[5,256,128]{2,1,0:T(8,128)(2,1)} custom-call(s32[4,8]{1,0:T(4,128)} %pad_add_fusion.tables, bf16[5,256,128]{2,1,0:T(8,128)(2,1)} %fusion.7.q_ref, s32[256,1]{1,0:T(8,128)} %copy.38.o_ref, s32[256,1]{1,0:T(8,128)} %copy.39.rs_ref, f32[1280,1]{1,0:T(8,128)} %get-tuple-element.16.top_ref, f32[1280,1]{1,0:T(8,128)} %get-tuple-element.17.total_ref, ...), custom_call_target="tpu_custom_call" | custom-call | tf_op jit(solution)/shard_map/pallas_call | solution.py:163
  173.0 6.6 %fusion.27 = bf16[256,5120]{1,0:T(8,128)(2,1)} fusion(bf16[256,640]{0,1:T(8,128)(2,1)S(1)} %bitcast.72, bf16[640,5120]{1,0:T(8,128)(2,1)} %param.20), kind=kOutput, calls=%fused_computation.124 | convolution fusion | flops 1677721600 | bytes 9502720 | tf_op jit(solution)/shard_map/dot_general | solution.py:278
  179.6 4.5 %all-to-all-start = ((bf16[4,32,32,2,128]{4,3,2,0,1:T(2,128)(2,1)}), bf16[4,32,32,2,128]{4,3,2,0,1:T(2,128)(2,1)S(1)}, u32[]{:S(2)}, u32[]{:S(2)}) async-start(bf16[4,32,32,2,128]{4,3,2,0,1:T(2,128)(2,1)} %fusion.3), calls=%async_computation | async-start | bytes 4194304 | tf_op jit(solution)/shard_map/all_to_all | solution.py:280
  184.1 2.8 %fusion.2 = bf16[256,5120]{1,0:T(8,128)(2,1)S(1)} fusion(s32[]{:T(128)S(6)} %select_n.203, bf16[256,5120]{1,0:T(8,128)(2,1)} %fusion.27), kind=kLoop, calls=%fused_computation.19 | loop fusion | flops 5242880 | bytes 5242884 | tf_op jit(solution)/shard_map/concatenate | solution.py:172
  187.2 4.4 %collective-permute-start.13 = (bf16[256,640]{1,0:T(8,128)(2,1)S(1)}, bf16[256,640]{1,0:T(8,128)(2,1)S(1)}, u32[]{:S(2)}, u32[]{:S(2)}) collective-permute-start(bf16[256,640]{1,0:T(8,128)(2,1)S(1)} %get-tuple-element.31), channel_id=1, source_target_pairs={{0,7},{1,0},{2,1},{3,2},{4,3},{5,4},{6,5},{7,6},{8,15},{9,8},{10,9... | collective-permute-start | bytes 983048 | tf_op jit(solution)/shard_map/ppermute | solution.py:197
  193.1 3.1 %collective-permute-start.10 = (bf16[256,640]{1,0:T(8,128)(2,1)S(1)}, bf16[256,640]{1,0:T(8,128)(2,1)S(1)}, u32[]{:S(2)}, u32[]{:S(2)}) collective-permute-start(bf16[256,640]{1,0:T(8,128)(2,1)S(1)} %get-tuple-element.28), channel_id=1, source_target_pairs={{0,4},{1,5},{2,6},{3,7},{4,0},{5,1},{6,2},{7,3},{8,12},{9,13},{10,... | collective-permute-start | bytes 983048 | tf_op jit(solution)/shard_map/ppermute | solution.py:197
  197.3 24.9 %collective-permute-done.13 = bf16[256,640]{1,0:T(8,128)(2,1)S(1)} collective-permute-done((bf16[256,640]{1,0:T(8,128)(2,1)S(1)}, bf16[256,640]{1,0:T(8,128)(2,1)S(1)}, u32[]{:S(2)}, u32[]{:S(2)}) %collective-permute-start.13) | collective-permute-done | bytes 327712 | tf_op jit(solution)/shard_map/ppermute | solution.py:197
  222.2 9.0 %collective-permute-start.7 = (bf16[256,640]{1,0:T(8,128)(2,1)S(1)}, bf16[256,640]{1,0:T(8,128)(2,1)S(1)}, u32[]{:S(2)}, u32[]{:S(2)}) collective-permute-start(bf16[256,640]{1,0:T(8,128)(2,1)S(1)} %get-tuple-element.25), channel_id=1, source_target_pairs={{0,1},{1,2},{2,3},{3,4},{4,5},{5,6},{6,7},{7,0},{8,9},{9,10},{10,1... | collective-permute-start | bytes 983048 | tf_op jit(solution)/shard_map/ppermute | solution.py:197
  231.2 9.1 %collective-permute-done.8 = bf16[256,640]{1,0:T(8,128)(2,1)S(1)} collective-permute-done((bf16[256,640]{1,0:T(8,128)(2,1)S(1)}, bf16[256,640]{1,0:T(8,128)(2,1)S(1)}, u32[]{:S(2)}, u32[]{:S(2)}) %collective-permute-start.8) | collective-permute-done | bytes 327712 | tf_op jit(solution)/shard_map/ppermute | solution.py:197
  240.2 4.4 %collective-permute-done.7 = bf16[256,640]{1,0:T(8,128)(2,1)S(1)} collective-permute-done((bf16[256,640]{1,0:T(8,128)(2,1)S(1)}, bf16[256,640]{1,0:T(8,128)(2,1)S(1)}, u32[]{:S(2)}, u32[]{:S(2)}) %collective-permute-start.7) | collective-permute-done | bytes 327712 | tf_op jit(solution)/shard_map/ppermute | solution.py:197
  245.7 4.0 %copy.43 = bf16[4,16,2,32,2,128]{5,4,3,1,2,0:T(2,128)(2,1)} copy(bf16[4,16,2,32,2,128]{5,4,3,0,2,1:T(2,128)(2,1)S(1)} %bitcast.69) | data formatting | bytes 4194304 | tf_op jit(solution)/shard_map/all_to_all | solution.py:280
  (119 shorter events, 36.6 us)
Async XLA Ops:
  7.2 78.8 %copy-start = (bf16[5120,128]{1,0:T(8,128)(2,1)S(1)}, bf16[5120,128]{1,0:T(8,128)(2,1)}, u32[]{:S(2)}) copy-start(bf16[5120,128]{1,0:T(8,128)(2,1)} %param.19) | copy-start | bytes 3932164
  7.2 22.2 %copy-start.6 = (s32[12]{0:T(128)S(1)}, s32[12]{0:T(128)}, u32[]{:S(2)}) copy-start(s32[12]{0:T(128)} %param.14) | copy-start | bytes 148
  7.2 24.2 %copy-start.7 = (s32[32]{0:T(128)S(1)}, s32[32]{0:T(128)}, u32[]{:S(2)}) copy-start(s32[32]{0:T(128)} %param.16) | copy-start | bytes 388
  7.2 76.2 %all-gather.4.cloned.1.call-start = ((), (), s32[]{:S(2)}) async-start(), calls=%async_computation.1 | async-start | bytes 6684672 | tf_op jit(solution)/shard_map/all_gather | solution.py:225
  9.8 28.9 %copy-start.4 = (s32[4096]{0:T(1024)S(1)}, s32[4096]{0:T(1024)}, u32[]{:S(2)}) copy-start(s32[4096]{0:T(1024)} %param.13) | copy-start | bytes 49156
  12.3 113.7 %all-gather.6.cloned.1.call-start = ((), (), s32[]{:S(2)}) async-start(), calls=%async_computation.2 | async-start | bytes 2228224 | tf_op jit(solution)/shard_map/all_gather | solution.py:258
  12.3 36.6 %collective-permute-start = (bf16[256,640]{1,0:T(8,128)(2,1)}, bf16[256,640]{1,0:T(8,128)(2,1)}, u32[]{:S(2)}, u32[]{:S(2)}) collective-permute-start(bf16[256,640]{1,0:T(8,128)(2,1)} %param.12), channel_id=1, source_target_pairs={{0,7},{1,0},{2,1},{3,2},{4,3},{5,4},{6,5},{7,6},{8,15},{9,8},{10,9... | collective-permute-start | bytes 983048 | tf_op jit(solution)/shard_map/ppermute | solution.py:182
  18.8 34.6 %collective-permute-start.1 = (bf16[256,640]{1,0:T(8,128)(2,1)}, bf16[256,640]{1,0:T(8,128)(2,1)}, u32[]{:S(2)}, u32[]{:S(2)}) collective-permute-start(bf16[256,640]{1,0:T(8,128)(2,1)} %param.12), channel_id=1, source_target_pairs={{0,6},{1,7},{2,0},{3,1},{4,2},{5,3},{6,4},{7,5},{8,14},{9,15},{10,... | collective-permute-start | bytes 983048 | tf_op jit(solution)/shard_map/ppermute | solution.py:182
  19.5 35.3 %collective-permute-start.2 = (bf16[256,640]{1,0:T(8,128)(2,1)}, bf16[256,640]{1,0:T(8,128)(2,1)}, u32[]{:S(2)}, u32[]{:S(2)}) collective-permute-start(bf16[256,640]{1,0:T(8,128)(2,1)} %param.12), channel_id=1, source_target_pairs={{0,5},{1,6},{2,7},{3,0},{4,1},{5,2},{6,3},{7,4},{8,13},{9,14},{10,... | collective-permute-start | bytes 983048 | tf_op jit(solution)/shard_map/ppermute | solution.py:182
  19.5 36.3 %collective-permute-start.3 = (bf16[256,640]{1,0:T(8,128)(2,1)}, bf16[256,640]{1,0:T(8,128)(2,1)}, u32[]{:S(2)}, u32[]{:S(2)}) collective-permute-start(bf16[256,640]{1,0:T(8,128)(2,1)} %param.12), channel_id=1, source_target_pairs={{0,4},{1,5},{2,6},{3,7},{4,0},{5,1},{6,2},{7,3},{8,12},{9,13},{10,... | collective-permute-start | bytes 983048 | tf_op jit(solution)/shard_map/ppermute | solution.py:182
  23.4 33.4 %collective-permute-start.4 = (bf16[256,640]{1,0:T(8,128)(2,1)}, bf16[256,640]{1,0:T(8,128)(2,1)}, u32[]{:S(2)}, u32[]{:S(2)}) collective-permute-start(bf16[256,640]{1,0:T(8,128)(2,1)} %param.12), channel_id=1, source_target_pairs={{0,3},{1,4},{2,5},{3,6},{4,7},{5,0},{6,1},{7,2},{8,11},{9,12},{10,... | collective-permute-start | bytes 983048 | tf_op jit(solution)/shard_map/ppermute | solution.py:182
  44.5 9.0 %copy-start.3 = (bf16[256,640]{1,0:T(8,128)(2,1)S(1)}, bf16[256,640]{1,0:T(8,128)(2,1)}, u32[]{:S(2)}) copy-start(bf16[256,640]{1,0:T(8,128)(2,1)} %param.12) | copy-start | bytes 983044
  49.0 15.2 %collective-permute-start.5 = (bf16[256,640]{1,0:T(8,128)(2,1)}, bf16[256,640]{1,0:T(8,128)(2,1)S(1)}, u32[]{:S(2)}, u32[]{:S(2)}) collective-permute-start(bf16[256,640]{1,0:T(8,128)(2,1)} %param.12), channel_id=1, source_target_pairs={{0,2},{1,3},{2,4},{3,5},{4,6},{5,7},{6,0},{7,1},{8,10},{9,11},{10,... | collective-permute-start | bytes 983048 | tf_op jit(solution)/shard_map/ppermute | solution.py:182
  53.5 15.5 %collective-permute-start.6 = (bf16[256,640]{1,0:T(8,128)(2,1)S(1)}, bf16[256,640]{1,0:T(8,128)(2,1)S(1)}, u32[]{:S(2)}, u32[]{:S(2)}) collective-permute-start(bf16[256,640]{1,0:T(8,128)(2,1)S(1)} %copy-done.3), channel_id=1, source_target_pairs={{0,1},{1,2},{2,3},{3,4},{4,5},{5,6},{6,7},{7,0},{8,9},{9,10},{10,1... | collective-permute-start | bytes 983048 | tf_op jit(solution)/shard_map/ppermute | solution.py:182
  74.4 14.4 %copy-start.5 = (bf16[5120,128]{1,0:T(8,128)(2,1)S(1)}, bf16[5120,128]{1,0:T(8,128)(2,1)}, u32[]{:S(2)}) copy-start(bf16[5120,128]{1,0:T(8,128)(2,1)} %param.18) | copy-start | bytes 3932164
  83.4 5.3 %copy-start.2 = (bf16[256,5120]{1,0:T(8,128)(2,1)S(1)}, bf16[256,5120]{1,0:T(8,128)(2,1)}, u32[]{:S(2)}) copy-start(bf16[256,5120]{1,0:T(8,128)(2,1)} %constant_dynamic-slice_fusion) | copy-start | bytes 7864324
  179.6 66.1 %all-to-all-start = ((bf16[4,32,32,2,128]{4,3,2,0,1:T(2,128)(2,1)}), bf16[4,32,32,2,128]{4,3,2,0,1:T(2,128)(2,1)S(1)}, u32[]{:S(2)}, u32[]{:S(2)}) async-start(bf16[4,32,32,2,128]{4,3,2,0,1:T(2,128)(2,1)} %fusion.3), calls=%async_computation | async-start | bytes 4194304 | tf_op jit(solution)/shard_map/all_to_all | solution.py:280
  184.1 65.6 %copy-start.1 = (bf16[5120,128]{1,0:T(8,128)(2,1)S(1)}, bf16[5120,128]{1,0:T(8,128)(2,1)}, u32[]{:S(2)}) copy-start(bf16[5120,128]{1,0:T(8,128)(2,1)} %param.19) | copy-start | bytes 3932164
  187.2 35.0 %collective-permute-start.13 = (bf16[256,640]{1,0:T(8,128)(2,1)S(1)}, bf16[256,640]{1,0:T(8,128)(2,1)S(1)}, u32[]{:S(2)}, u32[]{:S(2)}) collective-permute-start(bf16[256,640]{1,0:T(8,128)(2,1)S(1)} %get-tuple-element.31), channel_id=1, source_target_pairs={{0,7},{1,0},{2,1},{3,2},{4,3},{5,4},{6,5},{7,6},{8,15},{9,8},{10,9... | collective-permute-start | bytes 983048 | tf_op jit(solution)/shard_map/ppermute | solution.py:197
  191.5 30.7 %collective-permute-start.12 = (bf16[256,640]{1,0:T(8,128)(2,1)S(1)}, bf16[256,640]{1,0:T(8,128)(2,1)S(1)}, u32[]{:S(2)}, u32[]{:S(2)}) collective-permute-start(bf16[256,640]{1,0:T(8,128)(2,1)S(1)} %get-tuple-element.26), channel_id=1, source_target_pairs={{0,6},{1,7},{2,0},{3,1},{4,2},{5,3},{6,4},{7,5},{8,14},{9,15},{10,... | collective-permute-start | bytes 983048 | tf_op jit(solution)/shard_map/ppermute | solution.py:197
  192.3 38.9 %collective-permute-start.11 = (bf16[256,640]{1,0:T(8,128)(2,1)S(1)}, bf16[256,640]{1,0:T(8,128)(2,1)S(1)}, u32[]{:S(2)}, u32[]{:S(2)}) collective-permute-start(bf16[256,640]{1,0:T(8,128)(2,1)S(1)} %get-tuple-element.27), channel_id=1, source_target_pairs={{0,5},{1,6},{2,7},{3,0},{4,1},{5,2},{6,3},{7,4},{8,13},{9,14},{10,... | collective-permute-start | bytes 983048 | tf_op jit(solution)/shard_map/ppermute | solution.py:197
  193.1 38.1 %collective-permute-start.10 = (bf16[256,640]{1,0:T(8,128)(2,1)S(1)}, bf16[256,640]{1,0:T(8,128)(2,1)S(1)}, u32[]{:S(2)}, u32[]{:S(2)}) collective-permute-start(bf16[256,640]{1,0:T(8,128)(2,1)S(1)} %get-tuple-element.28), channel_id=1, source_target_pairs={{0,4},{1,5},{2,6},{3,7},{4,0},{5,1},{6,2},{7,3},{8,12},{9,13},{10,... | collective-permute-start | bytes 983048 | tf_op jit(solution)/shard_map/ppermute | solution.py:197
  196.2 35.0 %collective-permute-start.9 = (bf16[256,640]{1,0:T(8,128)(2,1)S(1)}, bf16[256,640]{1,0:T(8,128)(2,1)S(1)}, u32[]{:S(2)}, u32[]{:S(2)}) collective-permute-start(bf16[256,640]{1,0:T(8,128)(2,1)S(1)} %get-tuple-element.29), channel_id=1, source_target_pairs={{0,3},{1,4},{2,5},{3,6},{4,7},{5,0},{6,1},{7,2},{8,11},{9,12},{10,... | collective-permute-start | bytes 983048 | tf_op jit(solution)/shard_map/ppermute | solution.py:197
  222.2 18.1 %collective-permute-start.8 = (bf16[256,640]{1,0:T(8,128)(2,1)S(1)}, bf16[256,640]{1,0:T(8,128)(2,1)S(1)}, u32[]{:S(2)}, u32[]{:S(2)}) collective-permute-start(bf16[256,640]{1,0:T(8,128)(2,1)S(1)} %get-tuple-element.30), channel_id=1, source_target_pairs={{0,2},{1,3},{2,4},{3,5},{4,6},{5,7},{6,0},{7,1},{8,10},{9,11},{10,... | collective-permute-start | bytes 983048 | tf_op jit(solution)/shard_map/ppermute | solution.py:197
  222.2 22.4 %collective-permute-start.7 = (bf16[256,640]{1,0:T(8,128)(2,1)S(1)}, bf16[256,640]{1,0:T(8,128)(2,1)S(1)}, u32[]{:S(2)}, u32[]{:S(2)}) collective-permute-start(bf16[256,640]{1,0:T(8,128)(2,1)S(1)} %get-tuple-element.25), channel_id=1, source_target_pairs={{0,1},{1,2},{2,3},{3,4},{4,5},{5,6},{6,7},{7,0},{8,9},{9,10},{10,1... | collective-permute-start | bytes 983048 | tf_op jit(solution)/shard_map/ppermute | solution.py:197
Sparse Core Ops, SparseCore 0:
  12.4 70.9 all-gather.3
  91.1 34.9 all-gather.5

commit v3 on v2

--- a/solution.py
+++ b/solution.py
@@ -42,7 +42,7 @@
 from jax.experimental import pallas as pl
 from jax.experimental.pallas import tpu as pltpu
 
-TILE = 32
+TILE = 16
 CHUNK = 256
 
 
@@ -53,8 +53,7 @@
     scores = scores.reshape(-1, mask.shape[0], width)
     scores = jnp.where(mask[None], scores, -1e30).reshape(q.shape[0], width)
     new_top = jnp.maximum(top, jnp.max(scores, axis=1, keepdims=True))
-    expo = jnp.exp(scores - new_top).reshape(-1, mask.shape[0], width)
-    expo = jnp.where(mask[None], expo, 0.0).reshape(q.shape[0], width)
+    expo = jnp.exp(scores - new_top)
     fade = jnp.exp(top - new_top)
     total = total * fade + jnp.sum(expo, axis=1, keepdims=True)
     accum = accum * fade + jnp.dot(expo.astype(jnp.bfloat16), values, preferred_element_type=jnp.float32)
@@ -256,6 +255,8 @@
         axis=2,
     ).reshape(rows, local_heads * 2 * HEAD_SIZE)
     gathered = lax.all_gather(fresh_rows, "seq", axis=0, tiled=True)
+    gathered, arranged = lax.optimization_barrier((gathered, arranged))
+    decode_cache = lax.all_to_all(arranged, "seq", split_axis=1, concat_axis=2, tiled=True)
     kv_sorted = jnp.take(gathered, by_order, axis=0)
     earlier = (my_order[None, :] < my_order[:, None]).astype(jnp.int32)
     unsort = jnp.sum(earlier, axis=1)
@@ -276,8 +277,6 @@
     outs = [jnp.take(result, unsort, axis=1).transpose(1, 0, 2) for result in outs]
     attn = jnp.stack(outs, axis=1).reshape(rows, local_heads * head_group * HEAD_SIZE)
     partial_value = jnp.dot(attn, w_out, preferred_element_type=jnp.float32)
-    partial_value, arranged = lax.optimization_barrier((partial_value, arranged))
-    decode_cache = lax.all_to_all(arranged, "seq", split_axis=1, concat_axis=2, tiled=True)
     attn_out = scatter_heads(partial_value)
     return (attn_out, decode_cache)
 

time: 256 us -> 261 us (1.020)
  Pallas kernels: 40.3 us -> 47 us
  waiting for transfers between devices: 57 us -> 54.3 us
    all_to_all x1, starting transfers between devices: 4.48 us -> 8.21 us  [on_device(): lax.all_to_all(arranged, 'seq', split_axis=1, concat_axis=2, tiled=True)]
    pallas_call x1, Pallas kernels: 18.9 us -> 22.3 us  [cache_attention(): pl.pallas_call(body, grid_spec=spec, out_shape=[jax.ShapeDtypeStruct((gro...]
    pallas_call x1, Pallas kernels: 21.4 us -> 24.7 us  [fresh_attention(): pl.pallas_call(body, grid_spec=spec, out_shape=jax.ShapeDtypeStruct(q_sor...]
    optimization_barrier x0 -> x1, local copies, waits for them, and re-layouts: none -> 3.28 us  [on_device(): gathered, arranged = lax.optimization_barrier((gathered, arranged))]
    all_gather x1 -> x0, local copies, waits for them, and re-layouts: 3.27 us -> none  [on_device(): gathered = lax.all_gather(fresh_rows, 'seq', axis=0, tiled=True)]
  transfers between devices with their start and end apart: 17 -> 17, of which waited for: 7 -> 7; matrix products, arithmetic and copies ran while one was open for 22% -> 24% of each run, Pallas kernels for 7% -> 9%
where the time goes in v3:
time: 261 us; the launch traced here: 260 us
  local copies, waits for them, and re-layouts  64.7 us (25%)
  waiting for transfers between devices  54.3 us (21%)
  Pallas kernels  47 us (18%)
  starting transfers between devices  40.4 us (15%)
  other arithmetic  23.1 us (9%)
  matrix products  15.6 us (6%)
  between operations  14.6 us (6%)
    ppermute x7, waiting for transfers between devices, scatter_heads(): total = total + lax.ppermute(piece, 'heads', pairs).astype(jnp.float32)  36 us
    pallas_call x1, Pallas kernels, fresh_attention(): pl.pallas_call(body, grid_spec=spec, out_shape=jax.ShapeDtypeStruct(q_sor...  24.7 us
    pallas_call x1, Pallas kernels, cache_attention(): pl.pallas_call(body, grid_spec=spec, out_shape=[jax.ShapeDtypeStruct((gro...  22.3 us
    ppermute x7, starting transfers between devices, scatter_heads(): total = total + lax.ppermute(piece, 'heads', pairs).astype(jnp.float32)  17.3 us
    gather x1, local copies, waits for them, and re-layouts, on_device(): kv_sorted = jnp.take(gathered, by_order, axis=0)  17 us
    ppermute x7, starting transfers between devices, gather_heads(): got[shift] = lax.ppermute(piece, 'heads', pairs)  14.7 us
    unnamed x34, local copies, waits for them, and re-layouts  13.3 us
    ppermute x7, waiting for transfers between devices, gather_heads(): got[shift] = lax.ppermute(piece, 'heads', pairs)  11 us
  transfers between devices with their start and end apart: 17, of which 7 were waited for; matrix products, arithmetic and copies ran while one was open for 24% of the time, Pallas kernels for 9%

profile of v3, /device:TPU:0, one launch (start us, length us, event | category | flops | bytes accessed | tf_op | source)
XLA Modules:
  0.0 259.8 jit_solution(9777777775115894476)
XLA Ops:
  12.3 6.5 %collective-permute-start = (bf16[256,640]{1,0:T(8,128)(2,1)}, bf16[256,640]{1,0:T(8,128)(2,1)}, u32[]{:S(2)}, u32[]{:S(2)}) collective-permute-start(bf16[256,640]{1,0:T(8,128)(2,1)} %param.12), channel_id=1, source_target_pairs={{0,7},{1,0},{2,1},{3,2},{4,3},{5,4},{6,5},{7,6},{8,15},{9,8},{10,9... | collective-permute-start | bytes 983048 | tf_op jit(solution)/shard_map/ppermute | solution.py:181
  19.5 3.9 %collective-permute-start.3 = (bf16[256,640]{1,0:T(8,128)(2,1)}, bf16[256,640]{1,0:T(8,128)(2,1)}, u32[]{:S(2)}, u32[]{:S(2)}) collective-permute-start(bf16[256,640]{1,0:T(8,128)(2,1)} %param.12), channel_id=1, source_target_pairs={{0,4},{1,5},{2,6},{3,7},{4,0},{5,1},{6,2},{7,3},{8,12},{9,13},{10,... | collective-permute-start | bytes 983048 | tf_op jit(solution)/shard_map/ppermute | solution.py:181
  25.4 1.9 gather_fusion.11
  27.4 1.9 gather_fusion.9
  29.5 1.9 gather_fusion.10
  31.6 7.1 %gather_fusion.4 = bf16[32,4,32,2,128]{4,3,2,1,0:T(2,128)(2,1)S(1)} fusion(bf16[4,32,32,2,128]{4,3,2,1,0:T(2,128)(2,1)} %param.21, s32[1024]{0:T(1024)S(1)} %pad_clamp_fusion.3), kind=kCustom, calls=%fused_computation.7 | custom fusion | bytes 4194432 | tf_op jit(solution)/shard_map/jit(_take)/gather | solution.py:218
  38.7 5.8 %sort.17 = (s32[4096]{0:T(1024)}, s32[4096]{0:T(1024)S(1)}) sort(s32[4096]{0:T(1024)S(1)} %copy-done.4, s32[4096]{0:T(1024)S(1)} %iota.42), dimensions={0}, to_apply=%region_6.8 | sort | flops 49152 | bytes 65536 | tf_op jit(solution)/shard_map/jit(argsort)/sort | solution.py:225
  45.6 3.3 %fusion.3 = bf16[4,32,32,2,128]{4,3,2,0,1:T(2,128)(2,1)} fusion(bf16[32,4,32,2,128]{4,3,2,1,0:T(2,128)(2,1)S(1)} %gather_fusion.4, pred[32]{0:T(512)(128)(4,1)S(1)} %compare_and_fusion.3), kind=kLoop, calls=%fused_computation.21 | loop fusion | flops 1048576 | bytes 4194336 | tf_op jit(solution)/shard_map/jit(_take)/select_n | solution.py:218
  49.0 3.4 %collective-permute-start.5 = (bf16[256,640]{1,0:T(8,128)(2,1)}, bf16[256,640]{1,0:T(8,128)(2,1)S(1)}, u32[]{:S(2)}, u32[]{:S(2)}) collective-permute-start(bf16[256,640]{1,0:T(8,128)(2,1)} %param.12), channel_id=1, source_target_pairs={{0,2},{1,3},{2,4},{3,5},{4,6},{5,7},{6,0},{7,1},{8,10},{9,11},{10,... | collective-permute-start | bytes 983048 | tf_op jit(solution)/shard_map/ppermute | solution.py:181
  57.9 6.3 %collective-permute-done.5 = bf16[256,640]{1,0:T(8,128)(2,1)S(1)} collective-permute-done((bf16[256,640]{1,0:T(8,128)(2,1)}, bf16[256,640]{1,0:T(8,128)(2,1)S(1)}, u32[]{:S(2)}, u32[]{:S(2)}) %collective-permute-start.5) | collective-permute-done | bytes 327712 | tf_op jit(solution)/shard_map/ppermute | solution.py:181
  64.2 4.7 %collective-permute-done.6 = bf16[256,640]{1,0:T(8,128)(2,1)S(1)} collective-permute-done((bf16[256,640]{1,0:T(8,128)(2,1)S(1)}, bf16[256,640]{1,0:T(8,128)(2,1)S(1)}, u32[]{:S(2)}, u32[]{:S(2)}) %collective-permute-start.6) | collective-permute-done | bytes 327712 | tf_op jit(solution)/shard_map/ppermute | solution.py:181
  74.4 1.7 constant_dynamic-slice_fusion
  76.1 7.3 %all-gather.4.cloned.1.call-done.cache_ref = bf16[24,512,256]{2,1,0:T(8,128)(2,1)} async-done(((bf16[24,32,256]{2,1,0:T(8,128)(2,1)}), bf16[24,512,256]{2,1,0:T(8,128)(2,1)}) %all-gather.4.cloned.1.call-update) | async-done | bytes 6291472 | tf_op jit(solution)/shard_map/all_gather | solution.py:224
  83.4 2.5 fusion
  85.9 2.8 %fusion.4 = bf16[256,1,128]{0,2,1:T(8,128)(2,1)S(1)} fusion(bf16[5120,128]{1,0:T(8,128)(2,1)S(1)} %copy-done, bf16[256,5120]{1,0:T(8,128)(2,1)} %constant_dynamic-slice_fusion, f32[256]{0:T(256)S(1)} %add_rsqrt_fusion), kind=kOutput, calls=%fused_computation.25 | convolution fusion | flops 339509248 | bytes 3998720 | tf_op jit(solution)/shard_map/dot_general | solution.py:236
  97.2 6.5 %fusion.23 = f32[256,640]{0,1:T(8,128)S(1)} fusion(bf16[5120,640]{1,0:T(8,128)(2,1)} %param.17, bf16[256,5120]{1,0:T(8,128)(2,1)} %constant_dynamic-slice_fusion, f32[256]{0:T(256)S(1)} %add_rsqrt_fusion), kind=kOutput, calls=%fused_computation.122 | convolution fusion | flops 1681653760 | bytes 9831424 | tf_op jit(solution)/shard_map/dot_general | solution.py:234
  106.9 22.3 %shard_map.113 = (f32[1280,1]{1,0:T(8,128)}, f32[1280,1]{1,0:T(8,128)}, f32[1280,128]{1,0:T(8,128)}) custom-call(s32[4,16]{1,0:T(4,128)} %pad_add_fusion.tables, bf16[5,256,128]{2,1,0:T(8,128)(2,1)} %fusion.7.q_ref, s32[256,1]{1,0:T(8,128)} %copy.36.req_ref, bf16[24,512,256]{2,1,0:T(8,128)(2,1)} %all-gather.4.cloned.1.call-done.cache_ref), custom_call_target="tpu_custom_call" | custom-call | tf_op jit(solution)/shard_map/pallas_call | solution.py:130
  129.3 3.3 %copy.37 = bf16[4096,256]{1,0:T(8,128)(2,1)S(1)} copy(bf16[4096,256]{0,1:T(8,128)(2,1)} %bitcast.70) | data formatting | bytes 4194304 | tf_op jit(solution)/shard_map/optimization_barrier | solution.py:258
  132.6 17.0 %gather_fusion.7 = bf16[4096,256]{1,0:T(8,128)(2,1)} fusion(bf16[4096,256]{1,0:T(8,128)(2,1)S(1)} %copy.37, s32[4096]{0:T(1024)S(1)} %fusion.16), kind=kCustom, calls=%fused_computation.10 | custom fusion | bytes 4210688 | tf_op jit(solution)/shard_map/jit(_take)/gather | solution.py:260
  149.6 2.9 %broadcast_select_fusion.1.kv_ref = bf16[4096,256]{1,0:T(8,128)(2,1)} fusion(bf16[4096,256]{1,0:T(8,128)(2,1)} %gather_fusion.7, pred[4096]{0:T(1024)(128)(4,1)S(1)} %compare_and_fusion), kind=kLoop, calls=%fused_computation.22 | loop fusion | flops 1048576 | bytes 4198400 | tf_op jit(solution)/shard_map/jit(_take)/select_n | solution.py:260
  152.5 24.7 %shard_map.114 = bf16[5,256,128]{2,1,0:T(8,128)(2,1)} custom-call(s32[4,16]{1,0:T(4,128)} %pad_add_fusion.tables, bf16[5,256,128]{2,1,0:T(8,128)(2,1)} %fusion.7.q_ref, s32[256,1]{1,0:T(8,128)} %copy.38.o_ref, s32[256,1]{1,0:T(8,128)} %copy.39.rs_ref, f32[1280,1]{1,0:T(8,128)} %get-tuple-element.16.top_ref, f32[1280,1]{1,0:T(8,128)} %get-tuple-element.17.total_ref, ...), custom_call_target="tpu_custom_call" | custom-call | tf_op jit(solution)/shard_map/pallas_call | solution.py:162
  179.5 8.2 %all-to-all-start = ((bf16[4,32,32,2,128]{4,3,2,0,1:T(2,128)(2,1)}), bf16[4,32,32,2,128]{4,3,2,0,1:T(2,128)(2,1)S(1)}, u32[]{:S(2)}, u32[]{:S(2)}) async-start(bf16[4,32,32,2,128]{4,3,2,0,1:T(2,128)(2,1)} %fusion.3), calls=%async_computation | async-start | bytes 4194304 | tf_op jit(solution)/shard_map/all_to_all | solution.py:259
  187.8 5.1 %convolution_convert_fusion = bf16[256,5120]{1,0:T(8,128)(2,1)S(1)} fusion(bf16[256,640]{0,1:T(8,128)(2,1)S(1)} %bitcast.72, bf16[640,5120]{1,0:T(8,128)(2,1)} %param.20), kind=kOutput, calls=%fused_computation.14 | convolution fusion | flops 1679032320 | bytes 9502720 | tf_op jit(solution)/shard_map/dot_general | solution.py:279
  195.7 3.5 %collective-permute-start.12 = (bf16[256,640]{1,0:T(8,128)(2,1)S(1)}, bf16[256,640]{1,0:T(8,128)(2,1)S(1)}, u32[]{:S(2)}, u32[]{:S(2)}) collective-permute-start(bf16[256,640]{1,0:T(8,128)(2,1)S(1)} %get-tuple-element.26), channel_id=1, source_target_pairs={{0,6},{1,7},{2,0},{3,1},{4,2},{5,3},{6,4},{7,5},{8,14},{9,15},{10,... | collective-permute-start | bytes 983048 | tf_op jit(solution)/shard_map/ppermute | solution.py:196
  199.1 2.5 collective-permute-start.10
  201.6 3.2 %collective-permute-start.9 = (bf16[256,640]{1,0:T(8,128)(2,1)S(1)}, bf16[256,640]{1,0:T(8,128)(2,1)S(1)}, u32[]{:S(2)}, u32[]{:S(2)}) collective-permute-start(bf16[256,640]{1,0:T(8,128)(2,1)S(1)} %get-tuple-element.29), channel_id=1, source_target_pairs={{0,3},{1,4},{2,5},{3,6},{4,7},{5,0},{6,1},{7,2},{8,11},{9,12},{10,... | collective-permute-start | bytes 983048 | tf_op jit(solution)/shard_map/ppermute | solution.py:196
  204.8 22.1 %collective-permute-done.13 = bf16[256,640]{1,0:T(8,128)(2,1)S(1)} collective-permute-done((bf16[256,640]{1,0:T(8,128)(2,1)S(1)}, bf16[256,640]{1,0:T(8,128)(2,1)S(1)}, u32[]{:S(2)}, u32[]{:S(2)}) %collective-permute-start.13) | collective-permute-done | bytes 327712 | tf_op jit(solution)/shard_map/ppermute | solution.py:196
  226.9 7.0 %collective-permute-start.7 = (bf16[256,640]{1,0:T(8,128)(2,1)S(1)}, bf16[256,640]{1,0:T(8,128)(2,1)S(1)}, u32[]{:S(2)}, u32[]{:S(2)}) collective-permute-start(bf16[256,640]{1,0:T(8,128)(2,1)S(1)} %get-tuple-element.25), channel_id=1, source_target_pairs={{0,1},{1,2},{2,3},{3,4},{4,5},{5,6},{6,7},{7,0},{8,9},{9,10},{10,1... | collective-permute-start | bytes 983048 | tf_op jit(solution)/shard_map/ppermute | solution.py:196
  234.0 6.5 %collective-permute-done.9 = bf16[256,640]{1,0:T(8,128)(2,1)S(1)} collective-permute-done((bf16[256,640]{1,0:T(8,128)(2,1)S(1)}, bf16[256,640]{1,0:T(8,128)(2,1)S(1)}, u32[]{:S(2)}, u32[]{:S(2)}) %collective-permute-start.9) | collective-permute-done | bytes 327712 | tf_op jit(solution)/shard_map/ppermute | solution.py:196
  240.4 1.9 collective-permute-done.8
  242.3 5.5 %collective-permute-done.7 = bf16[256,640]{1,0:T(8,128)(2,1)S(1)} collective-permute-done((bf16[256,640]{1,0:T(8,128)(2,1)S(1)}, bf16[256,640]{1,0:T(8,128)(2,1)S(1)}, u32[]{:S(2)}, u32[]{:S(2)}) %collective-permute-start.7) | collective-permute-done | bytes 327712 | tf_op jit(solution)/shard_map/ppermute | solution.py:196
  248.9 4.0 %copy.43 = bf16[4,16,2,32,2,128]{5,4,3,1,2,0:T(2,128)(2,1)} copy(bf16[4,16,2,32,2,128]{5,4,3,0,2,1:T(2,128)(2,1)S(1)} %bitcast.69) | data formatting | bytes 4194304 | tf_op jit(solution)/shard_map/all_to_all | solution.py:259
  (119 shorter events, 37.8 us)
Async XLA Ops:
  7.2 78.8 %copy-start = (bf16[5120,128]{1,0:T(8,128)(2,1)S(1)}, bf16[5120,128]{1,0:T(8,128)(2,1)}, u32[]{:S(2)}) copy-start(bf16[5120,128]{1,0:T(8,128)(2,1)} %param.19) | copy-start | bytes 3932164
  7.2 22.2 %copy-start.6 = (s32[12]{0:T(128)S(1)}, s32[12]{0:T(128)}, u32[]{:S(2)}) copy-start(s32[12]{0:T(128)} %param.14) | copy-start | bytes 148
  7.2 24.2 %copy-start.7 = (s32[32]{0:T(128)S(1)}, s32[32]{0:T(128)}, u32[]{:S(2)}) copy-start(s32[32]{0:T(128)} %param.16) | copy-start | bytes 388
  7.2 76.2 %all-gather.4.cloned.1.call-start = ((), (), s32[]{:S(2)}) async-start(), calls=%async_computation.1 | async-start | bytes 6684672 | tf_op jit(solution)/shard_map/all_gather | solution.py:224
  9.8 28.9 %copy-start.4 = (s32[4096]{0:T(1024)S(1)}, s32[4096]{0:T(1024)}, u32[]{:S(2)}) copy-start(s32[4096]{0:T(1024)} %param.13) | copy-start | bytes 49156
  12.3 117.0 %all-gather.6.cloned.1.call-start = ((), (), s32[]{:S(2)}) async-start(), calls=%async_computation.2 | async-start | bytes 2228224 | tf_op jit(solution)/shard_map/all_gather | solution.py:257
  12.3 36.6 %collective-permute-start = (bf16[256,640]{1,0:T(8,128)(2,1)}, bf16[256,640]{1,0:T(8,128)(2,1)}, u32[]{:S(2)}, u32[]{:S(2)}) collective-permute-start(bf16[256,640]{1,0:T(8,128)(2,1)} %param.12), channel_id=1, source_target_pairs={{0,7},{1,0},{2,1},{3,2},{4,3},{5,4},{6,5},{7,6},{8,15},{9,8},{10,9... | collective-permute-start | bytes 983048 | tf_op jit(solution)/shard_map/ppermute | solution.py:181
  18.8 34.6 %collective-permute-start.1 = (bf16[256,640]{1,0:T(8,128)(2,1)}, bf16[256,640]{1,0:T(8,128)(2,1)}, u32[]{:S(2)}, u32[]{:S(2)}) collective-permute-start(bf16[256,640]{1,0:T(8,128)(2,1)} %param.12), channel_id=1, source_target_pairs={{0,6},{1,7},{2,0},{3,1},{4,2},{5,3},{6,4},{7,5},{8,14},{9,15},{10,... | collective-permute-start | bytes 983048 | tf_op jit(solution)/shard_map/ppermute | solution.py:181
  19.5 35.3 %collective-permute-start.2 = (bf16[256,640]{1,0:T(8,128)(2,1)}, bf16[256,640]{1,0:T(8,128)(2,1)}, u32[]{:S(2)}, u32[]{:S(2)}) collective-permute-start(bf16[256,640]{1,0:T(8,128)(2,1)} %param.12), channel_id=1, source_target_pairs={{0,5},{1,6},{2,7},{3,0},{4,1},{5,2},{6,3},{7,4},{8,13},{9,14},{10,... | collective-permute-start | bytes 983048 | tf_op jit(solution)/shard_map/ppermute | solution.py:181
  19.5 36.3 %collective-permute-start.3 = (bf16[256,640]{1,0:T(8,128)(2,1)}, bf16[256,640]{1,0:T(8,128)(2,1)}, u32[]{:S(2)}, u32[]{:S(2)}) collective-permute-start(bf16[256,640]{1,0:T(8,128)(2,1)} %param.12), channel_id=1, source_target_pairs={{0,4},{1,5},{2,6},{3,7},{4,0},{5,1},{6,2},{7,3},{8,12},{9,13},{10,... | collective-permute-start | bytes 983048 | tf_op jit(solution)/shard_map/ppermute | solution.py:181
  23.4 33.4 %collective-permute-start.4 = (bf16[256,640]{1,0:T(8,128)(2,1)}, bf16[256,640]{1,0:T(8,128)(2,1)}, u32[]{:S(2)}, u32[]{:S(2)}) collective-permute-start(bf16[256,640]{1,0:T(8,128)(2,1)} %param.12), channel_id=1, source_target_pairs={{0,3},{1,4},{2,5},{3,6},{4,7},{5,0},{6,1},{7,2},{8,11},{9,12},{10,... | collective-permute-start | bytes 983048 | tf_op jit(solution)/shard_map/ppermute | solution.py:181
  44.5 9.0 %copy-start.3 = (bf16[256,640]{1,0:T(8,128)(2,1)S(1)}, bf16[256,640]{1,0:T(8,128)(2,1)}, u32[]{:S(2)}) copy-start(bf16[256,640]{1,0:T(8,128)(2,1)} %param.12) | copy-start | bytes 983044
  49.0 15.2 %collective-permute-start.5 = (bf16[256,640]{1,0:T(8,128)(2,1)}, bf16[256,640]{1,0:T(8,128)(2,1)S(1)}, u32[]{:S(2)}, u32[]{:S(2)}) collective-permute-start(bf16[256,640]{1,0:T(8,128)(2,1)} %param.12), channel_id=1, source_target_pairs={{0,2},{1,3},{2,4},{3,5},{4,6},{5,7},{6,0},{7,1},{8,10},{9,11},{10,... | collective-permute-start | bytes 983048 | tf_op jit(solution)/shard_map/ppermute | solution.py:181
  53.4 15.5 %collective-permute-start.6 = (bf16[256,640]{1,0:T(8,128)(2,1)S(1)}, bf16[256,640]{1,0:T(8,128)(2,1)S(1)}, u32[]{:S(2)}, u32[]{:S(2)}) collective-permute-start(bf16[256,640]{1,0:T(8,128)(2,1)S(1)} %copy-done.3), channel_id=1, source_target_pairs={{0,1},{1,2},{2,3},{3,4},{4,5},{5,6},{6,7},{7,0},{8,9},{9,10},{10,1... | collective-permute-start | bytes 983048 | tf_op jit(solution)/shard_map/ppermute | solution.py:181
  74.4 14.4 %copy-start.5 = (bf16[5120,128]{1,0:T(8,128)(2,1)S(1)}, bf16[5120,128]{1,0:T(8,128)(2,1)}, u32[]{:S(2)}) copy-start(bf16[5120,128]{1,0:T(8,128)(2,1)} %param.18) | copy-start | bytes 3932164
  83.4 5.3 %copy-start.2 = (bf16[256,5120]{1,0:T(8,128)(2,1)S(1)}, bf16[256,5120]{1,0:T(8,128)(2,1)}, u32[]{:S(2)}) copy-start(bf16[256,5120]{1,0:T(8,128)(2,1)} %constant_dynamic-slice_fusion) | copy-start | bytes 7864324
  179.5 69.4 %all-to-all-start = ((bf16[4,32,32,2,128]{4,3,2,0,1:T(2,128)(2,1)}), bf16[4,32,32,2,128]{4,3,2,0,1:T(2,128)(2,1)S(1)}, u32[]{:S(2)}, u32[]{:S(2)}) async-start(bf16[4,32,32,2,128]{4,3,2,0,1:T(2,128)(2,1)} %fusion.3), calls=%async_computation | async-start | bytes 4194304 | tf_op jit(solution)/shard_map/all_to_all | solution.py:259
  192.9 60.1 %copy-start.1 = (bf16[5120,128]{1,0:T(8,128)(2,1)S(1)}, bf16[5120,128]{1,0:T(8,128)(2,1)}, u32[]{:S(2)}) copy-start(bf16[5120,128]{1,0:T(8,128)(2,1)} %param.19) | copy-start | bytes 3932164
  194.5 32.4 %collective-permute-start.13 = (bf16[256,640]{1,0:T(8,128)(2,1)S(1)}, bf16[256,640]{1,0:T(8,128)(2,1)S(1)}, u32[]{:S(2)}, u32[]{:S(2)}) collective-permute-start(bf16[256,640]{1,0:T(8,128)(2,1)S(1)} %get-tuple-element.31), channel_id=1, source_target_pairs={{0,7},{1,0},{2,1},{3,2},{4,3},{5,4},{6,5},{7,6},{8,15},{9,8},{10,9... | collective-permute-start | bytes 983048 | tf_op jit(solution)/shard_map/ppermute | solution.py:196
  195.7 31.2 %collective-permute-start.12 = (bf16[256,640]{1,0:T(8,128)(2,1)S(1)}, bf16[256,640]{1,0:T(8,128)(2,1)S(1)}, u32[]{:S(2)}, u32[]{:S(2)}) collective-permute-start(bf16[256,640]{1,0:T(8,128)(2,1)S(1)} %get-tuple-element.26), channel_id=1, source_target_pairs={{0,6},{1,7},{2,0},{3,1},{4,2},{5,3},{6,4},{7,5},{8,14},{9,15},{10,... | collective-permute-start | bytes 983048 | tf_op jit(solution)/shard_map/ppermute | solution.py:196
  199.1 34.8 %collective-permute-start.11 = (bf16[256,640]{1,0:T(8,128)(2,1)S(1)}, bf16[256,640]{1,0:T(8,128)(2,1)S(1)}, u32[]{:S(2)}, u32[]{:S(2)}) collective-permute-start(bf16[256,640]{1,0:T(8,128)(2,1)S(1)} %get-tuple-element.27), channel_id=1, source_target_pairs={{0,5},{1,6},{2,7},{3,0},{4,1},{5,2},{6,3},{7,4},{8,13},{9,14},{10,... | collective-permute-start | bytes 983048 | tf_op jit(solution)/shard_map/ppermute | solution.py:196
  199.1 34.8 %collective-permute-start.10 = (bf16[256,640]{1,0:T(8,128)(2,1)S(1)}, bf16[256,640]{1,0:T(8,128)(2,1)S(1)}, u32[]{:S(2)}, u32[]{:S(2)}) collective-permute-start(bf16[256,640]{1,0:T(8,128)(2,1)S(1)} %get-tuple-element.28), channel_id=1, source_target_pairs={{0,4},{1,5},{2,6},{3,7},{4,0},{5,1},{6,2},{7,3},{8,12},{9,13},{10,... | collective-permute-start | bytes 983048 | tf_op jit(solution)/shard_map/ppermute | solution.py:196
  201.6 38.8 %collective-permute-start.9 = (bf16[256,640]{1,0:T(8,128)(2,1)S(1)}, bf16[256,640]{1,0:T(8,128)(2,1)S(1)}, u32[]{:S(2)}, u32[]{:S(2)}) collective-permute-start(bf16[256,640]{1,0:T(8,128)(2,1)S(1)} %get-tuple-element.29), channel_id=1, source_target_pairs={{0,3},{1,4},{2,5},{3,6},{4,7},{5,0},{6,1},{7,2},{8,11},{9,12},{10,... | collective-permute-start | bytes 983048 | tf_op jit(solution)/shard_map/ppermute | solution.py:196
  226.9 15.4 %collective-permute-start.8 = (bf16[256,640]{1,0:T(8,128)(2,1)S(1)}, bf16[256,640]{1,0:T(8,128)(2,1)S(1)}, u32[]{:S(2)}, u32[]{:S(2)}) collective-permute-start(bf16[256,640]{1,0:T(8,128)(2,1)S(1)} %get-tuple-element.30), channel_id=1, source_target_pairs={{0,2},{1,3},{2,4},{3,5},{4,6},{5,7},{6,0},{7,1},{8,10},{9,11},{10,... | collective-permute-start | bytes 983048 | tf_op jit(solution)/shard_map/ppermute | solution.py:196
  226.9 20.9 %collective-permute-start.7 = (bf16[256,640]{1,0:T(8,128)(2,1)S(1)}, bf16[256,640]{1,0:T(8,128)(2,1)S(1)}, u32[]{:S(2)}, u32[]{:S(2)}) collective-permute-start(bf16[256,640]{1,0:T(8,128)(2,1)S(1)} %get-tuple-element.25), channel_id=1, source_target_pairs={{0,1},{1,2},{2,3},{3,4},{4,5},{5,6},{6,7},{7,0},{8,9},{9,10},{10,1... | collective-permute-start | bytes 983048 | tf_op jit(solution)/shard_map/ppermute | solution.py:196
Sparse Core Ops, SparseCore 0:
  12.4 70.9 all-gather.3
  91.1 35.0 all-gather.5

commit v4 on v3

--- a/solution.py
+++ b/solution.py
@@ -42,8 +42,8 @@
 from jax.experimental import pallas as pl
 from jax.experimental.pallas import tpu as pltpu
 
-TILE = 16
-CHUNK = 256
+TILE = 32
+CHUNK = 512
 
 
 def _online(q, keys, values, mask, carry, scale):
@@ -68,10 +68,8 @@
 
     def cached(r, carry):
         mask = req_row == r
-        for j in range(2):
-            block = cache_ref[2 * r + j]
-            carry = _online(q, block[:, :size], block[:, size:], mask, carry, scale)
-        return carry
+        block = jnp.concatenate([cache_ref[2 * r], cache_ref[2 * r + 1]], axis=0)
+        return _online(q, block[:, :size], block[:, size:], mask, carry, scale)
 
     carry = (
         jnp.full((group * rows, 1), -1e30, jnp.float32),

time: 261 us -> 248 us (0.950)
  Pallas kernels: 47 us -> 30.6 us
  waiting for transfers between devices: 54.3 us -> 61.7 us
  starting transfers between devices: 40.4 us -> 36.5 us
    pallas_call x1, Pallas kernels: 24.7 us -> 14.4 us  [fresh_attention(): pl.pallas_call(body, grid_spec=spec, out_shape=jax.ShapeDtypeStruct(q_sor...]
    pallas_call x1, Pallas kernels: 22.3 us -> 16.2 us  [cache_attention(): pl.pallas_call(body, grid_spec=spec, out_shape=[jax.ShapeDtypeStruct((gro...]
    ppermute x7, waiting for transfers between devices: 36 us -> 40.4 us  [scatter_heads(): total = total + lax.ppermute(piece, 'heads', pairs).astype(jnp.float32)]
    all_to_all x1, starting transfers between devices: 8.21 us -> 4.87 us  [on_device(): lax.all_to_all(arranged, 'seq', split_axis=1, concat_axis=2, tiled=True)]
    all_gather x1, waiting for transfers between devices: 0.02 us -> 2.94 us  [on_device(): gathered = lax.all_gather(fresh_rows, 'seq', axis=0, tiled=True)]
  transfers between devices with their start and end apart: 17 -> 17, of which waited for: 7 -> 8; matrix products, arithmetic and copies ran while one was open for 24% -> 25% of each run, Pallas kernels for 9% -> 7%
where the time goes in v4:
time: 248 us; the launch traced here: 247 us
  local copies, waits for them, and re-layouts  64.7 us (26%)
  waiting for transfers between devices  61.7 us (25%)
  starting transfers between devices  36.5 us (15%)
  Pallas kernels  30.6 us (12%)
  other arithmetic  23.1 us (9%)
  matrix products  15.6 us (6%)
  between operations  14.6 us (6%)
    ppermute x7, waiting for transfers between devices, scatter_heads(): total = total + lax.ppermute(piece, 'heads', pairs).astype(jnp.float32)  40.4 us
    gather x1, local copies, waits for them, and re-layouts, on_device(): kv_sorted = jnp.take(gathered, by_order, axis=0)  17 us
    ppermute x7, starting transfers between devices, scatter_heads(): total = total + lax.ppermute(piece, 'heads', pairs).astype(jnp.float32)  16.8 us
    pallas_call x1, Pallas kernels, cache_attention(): pl.pallas_call(body, grid_spec=spec, out_shape=[jax.ShapeDtypeStruct((gro...  16.2 us
    ppermute x7, starting transfers between devices, gather_heads(): got[shift] = lax.ppermute(piece, 'heads', pairs)  14.7 us
    pallas_call x1, Pallas kernels, fresh_attention(): pl.pallas_call(body, grid_spec=spec, out_shape=jax.ShapeDtypeStruct(q_sor...  14.4 us
    unnamed x34, local copies, waits for them, and re-layouts  13.3 us
    ppermute x7, waiting for transfers between devices, gather_heads(): got[shift] = lax.ppermute(piece, 'heads', pairs)  11 us
  transfers between devices with their start and end apart: 17, of which 8 were waited for; matrix products, arithmetic and copies ran while one was open for 25% of the time, Pallas kernels for 7%

profile of v4, /device:TPU:0, one launch (start us, length us, event | category | flops | bytes accessed | tf_op | source)
XLA Modules:
  0.0 246.8 jit_solution(518308688723170643)
XLA Ops:
  12.3 6.5 %collective-permute-start = (bf16[256,640]{1,0:T(8,128)(2,1)}, bf16[256,640]{1,0:T(8,128)(2,1)}, u32[]{:S(2)}, u32[]{:S(2)}) collective-permute-start(bf16[256,640]{1,0:T(8,128)(2,1)} %param.12), channel_id=1, source_target_pairs={{0,7},{1,0},{2,1},{3,2},{4,3},{5,4},{6,5},{7,6},{8,15},{9,8},{10,9... | collective-permute-start | bytes 983048 | tf_op jit(solution)/shard_map/ppermute | solution.py:179
  19.5 3.9 %collective-permute-start.3 = (bf16[256,640]{1,0:T(8,128)(2,1)}, bf16[256,640]{1,0:T(8,128)(2,1)}, u32[]{:S(2)}, u32[]{:S(2)}) collective-permute-start(bf16[256,640]{1,0:T(8,128)(2,1)} %param.12), channel_id=1, source_target_pairs={{0,4},{1,5},{2,6},{3,7},{4,0},{5,1},{6,2},{7,3},{8,12},{9,13},{10,... | collective-permute-start | bytes 983048 | tf_op jit(solution)/shard_map/ppermute | solution.py:179
  25.4 1.9 gather_fusion.11
  27.4 1.9 gather_fusion.9
  29.5 1.9 gather_fusion.10
  31.6 7.1 %gather_fusion.4 = bf16[32,4,32,2,128]{4,3,2,1,0:T(2,128)(2,1)S(1)} fusion(bf16[4,32,32,2,128]{4,3,2,1,0:T(2,128)(2,1)} %param.21, s32[1024]{0:T(1024)S(1)} %pad_clamp_fusion.3), kind=kCustom, calls=%fused_computation.7 | custom fusion | bytes 4194432 | tf_op jit(solution)/shard_map/jit(_take)/gather | solution.py:216
  38.7 5.8 %sort.17 = (s32[4096]{0:T(1024)}, s32[4096]{0:T(1024)S(1)}) sort(s32[4096]{0:T(1024)S(1)} %copy-done.4, s32[4096]{0:T(1024)S(1)} %iota.42), dimensions={0}, to_apply=%region_6.8 | sort | flops 49152 | bytes 65536 | tf_op jit(solution)/shard_map/jit(argsort)/sort | solution.py:223
  45.6 3.3 %fusion.3 = bf16[4,32,32,2,128]{4,3,2,0,1:T(2,128)(2,1)} fusion(bf16[32,4,32,2,128]{4,3,2,1,0:T(2,128)(2,1)S(1)} %gather_fusion.4, pred[32]{0:T(512)(128)(4,1)S(1)} %compare_and_fusion.3), kind=kLoop, calls=%fused_computation.21 | loop fusion | flops 1048576 | bytes 4194336 | tf_op jit(solution)/shard_map/jit(_take)/select_n | solution.py:216
  49.0 3.4 %collective-permute-start.5 = (bf16[256,640]{1,0:T(8,128)(2,1)}, bf16[256,640]{1,0:T(8,128)(2,1)S(1)}, u32[]{:S(2)}, u32[]{:S(2)}) collective-permute-start(bf16[256,640]{1,0:T(8,128)(2,1)} %param.12), channel_id=1, source_target_pairs={{0,2},{1,3},{2,4},{3,5},{4,6},{5,7},{6,0},{7,1},{8,10},{9,11},{10,... | collective-permute-start | bytes 983048 | tf_op jit(solution)/shard_map/ppermute | solution.py:179
  57.9 6.3 %collective-permute-done.5 = bf16[256,640]{1,0:T(8,128)(2,1)S(1)} collective-permute-done((bf16[256,640]{1,0:T(8,128)(2,1)}, bf16[256,640]{1,0:T(8,128)(2,1)S(1)}, u32[]{:S(2)}, u32[]{:S(2)}) %collective-permute-start.5) | collective-permute-done | bytes 327712 | tf_op jit(solution)/shard_map/ppermute | solution.py:179
  64.2 4.7 %collective-permute-done.6 = bf16[256,640]{1,0:T(8,128)(2,1)S(1)} collective-permute-done((bf16[256,640]{1,0:T(8,128)(2,1)S(1)}, bf16[256,640]{1,0:T(8,128)(2,1)S(1)}, u32[]{:S(2)}, u32[]{:S(2)}) %collective-permute-start.6) | collective-permute-done | bytes 327712 | tf_op jit(solution)/shard_map/ppermute | solution.py:179
  74.4 1.7 constant_dynamic-slice_fusion
  76.1 7.3 %all-gather.4.cloned.1.call-done.cache_ref = bf16[24,512,256]{2,1,0:T(8,128)(2,1)} async-done(((bf16[24,32,256]{2,1,0:T(8,128)(2,1)}), bf16[24,512,256]{2,1,0:T(8,128)(2,1)}) %all-gather.4.cloned.1.call-update) | async-done | bytes 6291472 | tf_op jit(solution)/shard_map/all_gather | solution.py:222
  83.4 2.5 %fusion = f32[256]{0:T(256)S(1)} fusion(bf16[256,5120]{1,0:T(8,128)(2,1)} %constant_dynamic-slice_fusion), kind=kLoop, calls=%fused_computation.15 | loop fusion | flops 3931904 | bytes 2622464 | tf_op jit(solution)/shard_map/reduce_sum | solution.py:227
  85.9 2.8 %fusion.4 = bf16[256,1,128]{0,2,1:T(8,128)(2,1)S(1)} fusion(bf16[5120,128]{1,0:T(8,128)(2,1)S(1)} %copy-done, bf16[256,5120]{1,0:T(8,128)(2,1)} %constant_dynamic-slice_fusion, f32[256]{0:T(256)S(1)} %add_rsqrt_fusion), kind=kOutput, calls=%fused_computation.25 | convolution fusion | flops 339509248 | bytes 3998720 | tf_op jit(solution)/shard_map/dot_general | solution.py:234
  97.2 6.5 %fusion.23 = f32[256,640]{0,1:T(8,128)S(1)} fusion(bf16[5120,640]{1,0:T(8,128)(2,1)} %param.17, bf16[256,5120]{1,0:T(8,128)(2,1)} %constant_dynamic-slice_fusion, f32[256]{0:T(256)S(1)} %add_rsqrt_fusion), kind=kOutput, calls=%fused_computation.122 | convolution fusion | flops 1681653760 | bytes 9831424 | tf_op jit(solution)/shard_map/dot_general | solution.py:232
  106.9 16.2 %shard_map.113 = (f32[1280,1]{1,0:T(8,128)}, f32[1280,1]{1,0:T(8,128)}, f32[1280,128]{1,0:T(8,128)}) custom-call(s32[4,8]{1,0:T(4,128)} %pad_add_fusion.tables, bf16[5,256,128]{2,1,0:T(8,128)(2,1)} %fusion.7.q_ref, s32[256,1]{1,0:T(8,128)} %copy.36.req_ref, bf16[24,512,256]{2,1,0:T(8,128)(2,1)} %all-gather.4.cloned.1.call-done.cache_ref), custom_call_target="tpu_custom_call" | custom-call | tf_op jit(solution)/shard_map/pallas_call | solution.py:128
  123.1 2.9 %all-gather.6.cloned.1.call-done = bf16[4096,1,256]{0,2,1:T(8,128)(2,1)} async-done(((bf16[256,1,256]{0,2,1:T(8,128)(2,1)}), bf16[4096,1,256]{0,2,1:T(8,128)(2,1)}) %all-gather.6.cloned.1.call-update) | async-done | bytes 2097168 | tf_op jit(solution)/shard_map/all_gather | solution.py:255
  126.0 3.3 %copy.37 = bf16[4096,256]{1,0:T(8,128)(2,1)S(1)} copy(bf16[4096,256]{0,1:T(8,128)(2,1)} %bitcast.70) | data formatting | bytes 4194304 | tf_op jit(solution)/shard_map/optimization_barrier | solution.py:256
  129.3 17.0 %gather_fusion.7 = bf16[4096,256]{1,0:T(8,128)(2,1)} fusion(bf16[4096,256]{1,0:T(8,128)(2,1)S(1)} %copy.37, s32[4096]{0:T(1024)S(1)} %fusion.16), kind=kCustom, calls=%fused_computation.10 | custom fusion | bytes 4210688 | tf_op jit(solution)/shard_map/jit(_take)/gather | solution.py:258
  146.3 2.9 %broadcast_select_fusion.1.kv_ref = bf16[4096,256]{1,0:T(8,128)(2,1)} fusion(bf16[4096,256]{1,0:T(8,128)(2,1)} %gather_fusion.7, pred[4096]{0:T(1024)(128)(4,1)S(1)} %compare_and_fusion), kind=kLoop, calls=%fused_computation.22 | loop fusion | flops 1048576 | bytes 4198400 | tf_op jit(solution)/shard_map/jit(_take)/select_n | solution.py:258
  149.2 14.4 %shard_map.114 = bf16[5,256,128]{2,1,0:T(8,128)(2,1)} custom-call(s32[4,8]{1,0:T(4,128)} %pad_add_fusion.tables, bf16[5,256,128]{2,1,0:T(8,128)(2,1)} %fusion.7.q_ref, s32[256,1]{1,0:T(8,128)} %copy.38.o_ref, s32[256,1]{1,0:T(8,128)} %copy.39.rs_ref, f32[1280,1]{1,0:T(8,128)} %get-tuple-element.16.top_ref, f32[1280,1]{1,0:T(8,128)} %get-tuple-element.17.total_ref, ...), custom_call_target="tpu_custom_call" | custom-call | tf_op jit(solution)/shard_map/pallas_call | solution.py:160
  165.9 4.9 %all-to-all-start = ((bf16[4,32,32,2,128]{4,3,2,0,1:T(2,128)(2,1)}), bf16[4,32,32,2,128]{4,3,2,0,1:T(2,128)(2,1)S(1)}, u32[]{:S(2)}, u32[]{:S(2)}) async-start(bf16[4,32,32,2,128]{4,3,2,0,1:T(2,128)(2,1)} %fusion.3), calls=%async_computation | async-start | bytes 4194304 | tf_op jit(solution)/shard_map/all_to_all | solution.py:257
  170.8 5.1 %convolution_convert_fusion = bf16[256,5120]{1,0:T(8,128)(2,1)S(1)} fusion(bf16[256,640]{0,1:T(8,128)(2,1)S(1)} %bitcast.72, bf16[640,5120]{1,0:T(8,128)(2,1)} %param.20), kind=kOutput, calls=%fused_computation.14 | convolution fusion | flops 1679032320 | bytes 9502720 | tf_op jit(solution)/shard_map/dot_general | solution.py:277
  177.6 5.1 %collective-permute-start.13 = (bf16[256,640]{1,0:T(8,128)(2,1)S(1)}, bf16[256,640]{1,0:T(8,128)(2,1)S(1)}, u32[]{:S(2)}, u32[]{:S(2)}) collective-permute-start(bf16[256,640]{1,0:T(8,128)(2,1)S(1)} %get-tuple-element.31), channel_id=1, source_target_pairs={{0,7},{1,0},{2,1},{3,2},{4,3},{5,4},{6,5},{7,6},{8,15},{9,8},{10,9... | collective-permute-start | bytes 983048 | tf_op jit(solution)/shard_map/ppermute | solution.py:194
  184.5 2.9 %collective-permute-start.10 = (bf16[256,640]{1,0:T(8,128)(2,1)S(1)}, bf16[256,640]{1,0:T(8,128)(2,1)S(1)}, u32[]{:S(2)}, u32[]{:S(2)}) collective-permute-start(bf16[256,640]{1,0:T(8,128)(2,1)S(1)} %get-tuple-element.28), channel_id=1, source_target_pairs={{0,4},{1,5},{2,6},{3,7},{4,0},{5,1},{6,2},{7,3},{8,12},{9,13},{10,... | collective-permute-start | bytes 983048 | tf_op jit(solution)/shard_map/ppermute | solution.py:194
  187.4 26.4 %collective-permute-done.13 = bf16[256,640]{1,0:T(8,128)(2,1)S(1)} collective-permute-done((bf16[256,640]{1,0:T(8,128)(2,1)S(1)}, bf16[256,640]{1,0:T(8,128)(2,1)S(1)}, u32[]{:S(2)}, u32[]{:S(2)}) %collective-permute-start.13) | collective-permute-done | bytes 327712 | tf_op jit(solution)/shard_map/ppermute | solution.py:194
  213.9 7.0 %collective-permute-start.7 = (bf16[256,640]{1,0:T(8,128)(2,1)S(1)}, bf16[256,640]{1,0:T(8,128)(2,1)S(1)}, u32[]{:S(2)}, u32[]{:S(2)}) collective-permute-start(bf16[256,640]{1,0:T(8,128)(2,1)S(1)} %get-tuple-element.25), channel_id=1, source_target_pairs={{0,1},{1,2},{2,3},{3,4},{4,5},{5,6},{6,7},{7,0},{8,9},{9,10},{10,1... | collective-permute-start | bytes 983048 | tf_op jit(solution)/shard_map/ppermute | solution.py:194
  220.9 6.5 %collective-permute-done.9 = bf16[256,640]{1,0:T(8,128)(2,1)S(1)} collective-permute-done((bf16[256,640]{1,0:T(8,128)(2,1)S(1)}, bf16[256,640]{1,0:T(8,128)(2,1)S(1)}, u32[]{:S(2)}, u32[]{:S(2)}) %collective-permute-start.9) | collective-permute-done | bytes 327712 | tf_op jit(solution)/shard_map/ppermute | solution.py:194
  227.4 2.0 collective-permute-done.8
  229.4 5.5 %collective-permute-done.7 = bf16[256,640]{1,0:T(8,128)(2,1)S(1)} collective-permute-done((bf16[256,640]{1,0:T(8,128)(2,1)S(1)}, bf16[256,640]{1,0:T(8,128)(2,1)S(1)}, u32[]{:S(2)}, u32[]{:S(2)}) %collective-permute-start.7) | collective-permute-done | bytes 327712 | tf_op jit(solution)/shard_map/ppermute | solution.py:194
  235.9 4.0 %copy.43 = bf16[4,16,2,32,2,128]{5,4,3,1,2,0:T(2,128)(2,1)} copy(bf16[4,16,2,32,2,128]{5,4,3,0,2,1:T(2,128)(2,1)S(1)} %bitcast.69) | data formatting | bytes 4194304 | tf_op jit(solution)/shard_map/all_to_all | solution.py:257
  (119 shorter events, 38.3 us)
Async XLA Ops:
  7.2 78.8 %copy-start = (bf16[5120,128]{1,0:T(8,128)(2,1)S(1)}, bf16[5120,128]{1,0:T(8,128)(2,1)}, u32[]{:S(2)}) copy-start(bf16[5120,128]{1,0:T(8,128)(2,1)} %param.19) | copy-start | bytes 3932164
  7.2 22.2 %copy-start.6 = (s32[12]{0:T(128)S(1)}, s32[12]{0:T(128)}, u32[]{:S(2)}) copy-start(s32[12]{0:T(128)} %param.14) | copy-start | bytes 148
  7.2 24.2 %copy-start.7 = (s32[32]{0:T(128)S(1)}, s32[32]{0:T(128)}, u32[]{:S(2)}) copy-start(s32[32]{0:T(128)} %param.16) | copy-start | bytes 388
  7.2 76.2 %all-gather.4.cloned.1.call-start = ((), (), s32[]{:S(2)}) async-start(), calls=%async_computation.1 | async-start | bytes 6684672 | tf_op jit(solution)/shard_map/all_gather | solution.py:222
  9.8 28.9 %copy-start.4 = (s32[4096]{0:T(1024)S(1)}, s32[4096]{0:T(1024)}, u32[]{:S(2)}) copy-start(s32[4096]{0:T(1024)} %param.13) | copy-start | bytes 49156
  12.3 113.7 %all-gather.6.cloned.1.call-start = ((), (), s32[]{:S(2)}) async-start(), calls=%async_computation.2 | async-start | bytes 2228224 | tf_op jit(solution)/shard_map/all_gather | solution.py:255
  12.3 36.6 %collective-permute-start = (bf16[256,640]{1,0:T(8,128)(2,1)}, bf16[256,640]{1,0:T(8,128)(2,1)}, u32[]{:S(2)}, u32[]{:S(2)}) collective-permute-start(bf16[256,640]{1,0:T(8,128)(2,1)} %param.12), channel_id=1, source_target_pairs={{0,7},{1,0},{2,1},{3,2},{4,3},{5,4},{6,5},{7,6},{8,15},{9,8},{10,9... | collective-permute-start | bytes 983048 | tf_op jit(solution)/shard_map/ppermute | solution.py:179
  18.8 34.6 %collective-permute-start.1 = (bf16[256,640]{1,0:T(8,128)(2,1)}, bf16[256,640]{1,0:T(8,128)(2,1)}, u32[]{:S(2)}, u32[]{:S(2)}) collective-permute-start(bf16[256,640]{1,0:T(8,128)(2,1)} %param.12), channel_id=1, source_target_pairs={{0,6},{1,7},{2,0},{3,1},{4,2},{5,3},{6,4},{7,5},{8,14},{9,15},{10,... | collective-permute-start | bytes 983048 | tf_op jit(solution)/shard_map/ppermute | solution.py:179
  19.5 35.3 %collective-permute-start.2 = (bf16[256,640]{1,0:T(8,128)(2,1)}, bf16[256,640]{1,0:T(8,128)(2,1)}, u32[]{:S(2)}, u32[]{:S(2)}) collective-permute-start(bf16[256,640]{1,0:T(8,128)(2,1)} %param.12), channel_id=1, source_target_pairs={{0,5},{1,6},{2,7},{3,0},{4,1},{5,2},{6,3},{7,4},{8,13},{9,14},{10,... | collective-permute-start | bytes 983048 | tf_op jit(solution)/shard_map/ppermute | solution.py:179
  19.5 36.3 %collective-permute-start.3 = (bf16[256,640]{1,0:T(8,128)(2,1)}, bf16[256,640]{1,0:T(8,128)(2,1)}, u32[]{:S(2)}, u32[]{:S(2)}) collective-permute-start(bf16[256,640]{1,0:T(8,128)(2,1)} %param.12), channel_id=1, source_target_pairs={{0,4},{1,5},{2,6},{3,7},{4,0},{5,1},{6,2},{7,3},{8,12},{9,13},{10,... | collective-permute-start | bytes 983048 | tf_op jit(solution)/shard_map/ppermute | solution.py:179
  23.4 33.4 %collective-permute-start.4 = (bf16[256,640]{1,0:T(8,128)(2,1)}, bf16[256,640]{1,0:T(8,128)(2,1)}, u32[]{:S(2)}, u32[]{:S(2)}) collective-permute-start(bf16[256,640]{1,0:T(8,128)(2,1)} %param.12), channel_id=1, source_target_pairs={{0,3},{1,4},{2,5},{3,6},{4,7},{5,0},{6,1},{7,2},{8,11},{9,12},{10,... | collective-permute-start | bytes 983048 | tf_op jit(solution)/shard_map/ppermute | solution.py:179
  44.5 9.0 %copy-start.3 = (bf16[256,640]{1,0:T(8,128)(2,1)S(1)}, bf16[256,640]{1,0:T(8,128)(2,1)}, u32[]{:S(2)}) copy-start(bf16[256,640]{1,0:T(8,128)(2,1)} %param.12) | copy-start | bytes 983044
  49.0 15.2 %collective-permute-start.5 = (bf16[256,640]{1,0:T(8,128)(2,1)}, bf16[256,640]{1,0:T(8,128)(2,1)S(1)}, u32[]{:S(2)}, u32[]{:S(2)}) collective-permute-start(bf16[256,640]{1,0:T(8,128)(2,1)} %param.12), channel_id=1, source_target_pairs={{0,2},{1,3},{2,4},{3,5},{4,6},{5,7},{6,0},{7,1},{8,10},{9,11},{10,... | collective-permute-start | bytes 983048 | tf_op jit(solution)/shard_map/ppermute | solution.py:179
  53.4 15.5 %collective-permute-start.6 = (bf16[256,640]{1,0:T(8,128)(2,1)S(1)}, bf16[256,640]{1,0:T(8,128)(2,1)S(1)}, u32[]{:S(2)}, u32[]{:S(2)}) collective-permute-start(bf16[256,640]{1,0:T(8,128)(2,1)S(1)} %copy-done.3), channel_id=1, source_target_pairs={{0,1},{1,2},{2,3},{3,4},{4,5},{5,6},{6,7},{7,0},{8,9},{9,10},{10,1... | collective-permute-start | bytes 983048 | tf_op jit(solution)/shard_map/ppermute | solution.py:179
  74.4 14.4 %copy-start.5 = (bf16[5120,128]{1,0:T(8,128)(2,1)S(1)}, bf16[5120,128]{1,0:T(8,128)(2,1)}, u32[]{:S(2)}) copy-start(bf16[5120,128]{1,0:T(8,128)(2,1)} %param.18) | copy-start | bytes 3932164
  83.4 5.3 %copy-start.2 = (bf16[256,5120]{1,0:T(8,128)(2,1)S(1)}, bf16[256,5120]{1,0:T(8,128)(2,1)}, u32[]{:S(2)}) copy-start(bf16[256,5120]{1,0:T(8,128)(2,1)} %constant_dynamic-slice_fusion) | copy-start | bytes 7864324
  165.9 70.0 %all-to-all-start = ((bf16[4,32,32,2,128]{4,3,2,0,1:T(2,128)(2,1)}), bf16[4,32,32,2,128]{4,3,2,0,1:T(2,128)(2,1)S(1)}, u32[]{:S(2)}, u32[]{:S(2)}) async-start(bf16[4,32,32,2,128]{4,3,2,0,1:T(2,128)(2,1)} %fusion.3), calls=%async_computation | async-start | bytes 4194304 | tf_op jit(solution)/shard_map/all_to_all | solution.py:257
  175.9 64.0 %copy-start.1 = (bf16[5120,128]{1,0:T(8,128)(2,1)S(1)}, bf16[5120,128]{1,0:T(8,128)(2,1)}, u32[]{:S(2)}) copy-start(bf16[5120,128]{1,0:T(8,128)(2,1)} %param.19) | copy-start | bytes 3932164
  177.6 36.3 %collective-permute-start.13 = (bf16[256,640]{1,0:T(8,128)(2,1)S(1)}, bf16[256,640]{1,0:T(8,128)(2,1)S(1)}, u32[]{:S(2)}, u32[]{:S(2)}) collective-permute-start(bf16[256,640]{1,0:T(8,128)(2,1)S(1)} %get-tuple-element.31), channel_id=1, source_target_pairs={{0,7},{1,0},{2,1},{3,2},{4,3},{5,4},{6,5},{7,6},{8,15},{9,8},{10,9... | collective-permute-start | bytes 983048 | tf_op jit(solution)/shard_map/ppermute | solution.py:194
  182.7 31.1 %collective-permute-start.12 = (bf16[256,640]{1,0:T(8,128)(2,1)S(1)}, bf16[256,640]{1,0:T(8,128)(2,1)S(1)}, u32[]{:S(2)}, u32[]{:S(2)}) collective-permute-start(bf16[256,640]{1,0:T(8,128)(2,1)S(1)} %get-tuple-element.26), channel_id=1, source_target_pairs={{0,6},{1,7},{2,0},{3,1},{4,2},{5,3},{6,4},{7,5},{8,14},{9,15},{10,... | collective-permute-start | bytes 983048 | tf_op jit(solution)/shard_map/ppermute | solution.py:194
  183.6 37.3 %collective-permute-start.11 = (bf16[256,640]{1,0:T(8,128)(2,1)S(1)}, bf16[256,640]{1,0:T(8,128)(2,1)S(1)}, u32[]{:S(2)}, u32[]{:S(2)}) collective-permute-start(bf16[256,640]{1,0:T(8,128)(2,1)S(1)} %get-tuple-element.27), channel_id=1, source_target_pairs={{0,5},{1,6},{2,7},{3,0},{4,1},{5,2},{6,3},{7,4},{8,13},{9,14},{10,... | collective-permute-start | bytes 983048 | tf_op jit(solution)/shard_map/ppermute | solution.py:194
  184.5 36.4 %collective-permute-start.10 = (bf16[256,640]{1,0:T(8,128)(2,1)S(1)}, bf16[256,640]{1,0:T(8,128)(2,1)S(1)}, u32[]{:S(2)}, u32[]{:S(2)}) collective-permute-start(bf16[256,640]{1,0:T(8,128)(2,1)S(1)} %get-tuple-element.28), channel_id=1, source_target_pairs={{0,4},{1,5},{2,6},{3,7},{4,0},{5,1},{6,2},{7,3},{8,12},{9,13},{10,... | collective-permute-start | bytes 983048 | tf_op jit(solution)/shard_map/ppermute | solution.py:194
  187.4 40.0 %collective-permute-start.9 = (bf16[256,640]{1,0:T(8,128)(2,1)S(1)}, bf16[256,640]{1,0:T(8,128)(2,1)S(1)}, u32[]{:S(2)}, u32[]{:S(2)}) collective-permute-start(bf16[256,640]{1,0:T(8,128)(2,1)S(1)} %get-tuple-element.29), channel_id=1, source_target_pairs={{0,3},{1,4},{2,5},{3,6},{4,7},{5,0},{6,1},{7,2},{8,11},{9,12},{10,... | collective-permute-start | bytes 983048 | tf_op jit(solution)/shard_map/ppermute | solution.py:194
  213.9 15.5 %collective-permute-start.8 = (bf16[256,640]{1,0:T(8,128)(2,1)S(1)}, bf16[256,640]{1,0:T(8,128)(2,1)S(1)}, u32[]{:S(2)}, u32[]{:S(2)}) collective-permute-start(bf16[256,640]{1,0:T(8,128)(2,1)S(1)} %get-tuple-element.30), channel_id=1, source_target_pairs={{0,2},{1,3},{2,4},{3,5},{4,6},{5,7},{6,0},{7,1},{8,10},{9,11},{10,... | collective-permute-start | bytes 983048 | tf_op jit(solution)/shard_map/ppermute | solution.py:194
  213.9 21.0 %collective-permute-start.7 = (bf16[256,640]{1,0:T(8,128)(2,1)S(1)}, bf16[256,640]{1,0:T(8,128)(2,1)S(1)}, u32[]{:S(2)}, u32[]{:S(2)}) collective-permute-start(bf16[256,640]{1,0:T(8,128)(2,1)S(1)} %get-tuple-element.25), channel_id=1, source_target_pairs={{0,1},{1,2},{2,3},{3,4},{4,5},{5,6},{6,7},{7,0},{8,9},{9,10},{10,1... | collective-permute-start | bytes 983048 | tf_op jit(solution)/shard_map/ppermute | solution.py:194
Sparse Core Ops, SparseCore 0:
  12.4 70.9 all-gather.3
  91.1 34.9 all-gather.5
